TPU v7x, 32 devices: a whole 2x2x4 slice. The times are simulated.
32 devices in a mesh: pulse: 16 (over z, x, core), range: 2 (over y).
Axes of the slice: x: 2, y: 2, z: 4, core: 2. Of those that a mesh axis runs over, the one named last changes fastest.
Arguments:
- echo: bfloat16 [32, 2, 32768], P('pulse', None, 'range'), may hold values from -6 to 6
- chirp_phase: float32 [256], replicated, may hold values from -0.5 to 201.5624
- rec_phase: float32 [2, 2048, 2], P('range', 'pulse'), may hold values from -3.140625 to 3.140625
- rec_start: int32 [2, 2048], P('range', 'pulse'), may hold values from 0 to 32256
- rec_owner: int32 [2, 2048, 1], P('range', 'pulse'), may hold values from 0 to 31; in each aligned block of 128 rows (0 to 127, 128 to 255, ..., all dimensions but the last counted through in order) at most 6 rows name the same one
- rec_row: int32 [2, 2048], P('range', 'pulse'), may hold values from 0 to 63
- rec_weight: float32 [2, 2048], P('range', 'pulse'), may hold values from 0.2 to 1
- rec_count: int32 [2, 16], P('range', 'pulse'), may hold values from 96 to 128, as said below
- prior: bfloat16 [512, 2, 1024], P('pulse', None, 'range'), may hold values from -6 to 6
- interp_weight: bfloat16 [64, 32], replicated, may hold values from -1 to 1
Outputs:
- tiles: float32 [1024, 2, 1024], P('pulse', None, 'range')
Inputs may be any that keep to these rules, and one draw needn't show every extreme that they name: `rec_owner`: in each aligned block of 128 record slots (one device's slots) no owner is named more than 6 times. Owner o is the tile of pulse index o // 2 and range index o % 2, 2 being the number of range devices. `rec_count`: some subimage has all 128 slots live.
All inputs are finite; a program needn't handle non-finite values.
Results may differ from a plain program's by a relative error of at most 0.0034.
Values may be sent and summed in bfloat16 or wider, within the bound.
No kernel may reach another device: no remote copies, remote signals or barrier semaphores. Data moves between devices by JAX's collectives and lax.ppermute only.
A program may use at most 64 MiB of HBM per device.

v0:
```python
import jax
import jax.numpy as jnp
from jax import lax
from jax.experimental import pallas as pl
from jax.experimental.pallas import tpu as pltpu
from jax.sharding import PartitionSpec as P

SEG = 512
LANE = 128
GROUP = 8


def chirp_matrix(chirp_phase):
    tap_count = chirp_phase.shape[0]
    tap_scale = 1.0 / jnp.sqrt(jnp.float32(tap_count))
    real_taps = jnp.cos(chirp_phase) * tap_scale
    imag_taps = jnp.sin(chirp_phase) * tap_scale

    def banded(values):
        padded = jnp.concatenate([values, jnp.zeros((tap_count + 1,), jnp.float32)])
        return (
            jnp.tile(padded, tap_count)[: 2 * tap_count * tap_count]
            .reshape(tap_count, 2 * tap_count)
            .T
        )

    real_band = banded(real_taps)[: tap_count + LANE, :LANE]
    imag_band = banded(imag_taps)[: tap_count + LANE, :LANE]
    upper = jnp.concatenate([real_band, -imag_band], axis=1)
    lower = jnp.concatenate([imag_band, real_band], axis=1)
    return jnp.concatenate([upper, lower], axis=0).astype(jnp.bfloat16)


def compress_chunks(echo_full, filter_matrix, chunk_total):
    pulses, planes, bin_count = echo_full.shape
    taps = filter_matrix.shape[0] // planes - LANE
    reach = taps // LANE
    padded = jnp.pad(
        echo_full, ((0, 0), (0, 0), (0, (chunk_total + reach) * LANE - bin_count))
    )
    chunks = padded.reshape(pulses, planes, chunk_total + reach, LANE)
    windows = jnp.concatenate(
        [chunks[:, :, lead : lead + chunk_total] for lead in range(reach + 1)], axis=3
    )
    windows = windows.transpose(0, 2, 1, 3).reshape(pulses * chunk_total, -1)
    filtered = jnp.dot(windows, filter_matrix, preferred_element_type=jnp.float32)
    filtered = lax.reduce_precision(filtered, 8, 7)
    return filtered.reshape(pulses, chunk_total, planes * LANE)


def records_kernel(starts_ref, slot_ref, coef_ref, prof_ref, info_ref, out_ref):
    slots = starts_ref.shape[0]
    owners = info_ref.shape[0]
    per_owner = out_ref.shape[0] // owners
    lane_ids = lax.broadcasted_iota(jnp.int32, (GROUP, LANE), 1)
    row_ids = lax.broadcasted_iota(jnp.int32, (GROUP, LANE), 0)
    out_ref[...] = jnp.zeros(out_ref.shape, out_ref.dtype)

    def put_info(o, carry):
        out_ref[o * per_owner + per_owner - 1] = info_ref[o]
        return carry

    lax.fori_loop(0, owners, put_info, 0)

    def record(j, carry):
        st = starts_ref[j]
        first = st // LANE
        off = st - first * LANE
        aligned = pl.multiple_of((first // GROUP) * GROUP, GROUP)
        lift = (2 * GROUP - (first - aligned)) % (2 * GROUP)
        parts = []
        for k in range(2):
            rows = prof_ref[k, pl.ds(aligned, 2 * GROUP), :]
            rows = pltpu.roll(rows, lift, 0)[:GROUP]
            parts.append((rows[:, :LANE], rows[:, LANE:]))
        (re0, im0), (re1, im1) = parts
        c0, s0, c1, s1, sc = (coef_ref[i, j] for i in range(5))
        out_re = ((c0 * re0 + c1 * re1) - (s0 * im0 + s1 * im1)) * sc
        out_im = ((c0 * im0 + c1 * im1) + (s0 * re0 + s1 * re1)) * sc
        turn = (LANE - off) % LANE
        keep = lane_ids < LANE - off
        shifted = []
        for z in (out_re, out_im):
            rot = pltpu.roll(z, turn, 1)
            shifted.append(jnp.where(keep, rot, pltpu.roll(rot, GROUP - 1, 0)))
        tile = jnp.where(
            row_ids < GROUP // 2, shifted[0], pltpu.roll(shifted[1], GROUP // 2, 0)
        )
        out_ref[slot_ref[j]] = tile.astype(out_ref.dtype)
        return carry

    lax.fori_loop(0, slots, record, 0, unroll=8)


def form_payload(prof, starts, slot_index, coef, info, slot_total):
    vmem = pl.BlockSpec(memory_space=pltpu.VMEM)
    smem = pl.BlockSpec(memory_space=pltpu.SMEM)
    return pl.pallas_call(
        records_kernel,
        out_shape=jax.ShapeDtypeStruct((slot_total, GROUP, LANE), jnp.bfloat16),
        in_specs=[smem, smem, smem, vmem, vmem],
        out_specs=vmem,
    )(starts, slot_index, coef, prof, info)


def on_device(
    echo,
    chirp_phase,
    rec_phase,
    rec_start,
    rec_owner,
    rec_row,
    rec_weight,
    rec_count,
    prior,
    interp_weight,
):
    pulse_count = lax.axis_size("pulse")
    range_count = lax.axis_size("range")
    owner_total = pulse_count * range_count
    axes = ("pulse", "range")

    slot_count = rec_start.shape[1]
    owners = rec_owner[0, :, 0]
    dest_rows = rec_row[0]
    out_rows = interp_weight.shape[0]
    capacity = max(2, 3 * slot_count // (2 * owner_total))
    per_owner = capacity + 1
    slot_total = owner_total * per_owner

    filter_matrix = chirp_matrix(chirp_phase)
    if range_count == 2:
        other = lax.ppermute(echo, "range", [(0, 1), (1, 0)])
        first = lax.axis_index("range") == 0
        raw_echo = jnp.where(
            first, jnp.concatenate([echo, other], axis=2), jnp.concatenate([other, echo], axis=2)
        )
    else:
        raw_echo = lax.all_gather(echo, "range", axis=2, tiled=True)
    pulses, planes, bin_total = raw_echo.shape
    chunk_total = bin_total // LANE + 2 * GROUP
    prof = compress_chunks(raw_echo, filter_matrix, chunk_total)

    starts = rec_start[0]
    phases = rec_phase[0]
    weights = rec_weight[0]
    live_mask = (jnp.arange(slot_count) < rec_count[0, 0]).astype(jnp.float32)
    scales = live_mask * weights / jnp.sqrt(jnp.float32(pulses))
    cosine = lax.reduce_precision(jnp.cos(phases), 8, 7)
    sine_part = lax.reduce_precision(jnp.sin(phases), 8, 7)
    coef = jnp.stack([cosine[:, 0], sine_part[:, 0], cosine[:, 1], sine_part[:, 1], scales])

    owner_marks = (owners[:, None] == jnp.arange(owner_total)[None, :]).astype(jnp.int32)
    earlier = jnp.cumsum(owner_marks, axis=0) - owner_marks
    slot_rank = jnp.sum(earlier * owner_marks, axis=1)
    slot_index = owners * per_owner + jnp.minimum(slot_rank, capacity - 1)
    slot_index = jnp.clip(slot_index, 0, slot_total - 1).astype(jnp.int32)
    info_pos = slot_rank * out_rows + dest_rows
    info = jnp.dot(
        owner_marks.T.astype(jnp.bfloat16),
        (info_pos[:, None] == jnp.arange(GROUP * LANE)[None, :]).astype(jnp.bfloat16),
        preferred_element_type=jnp.float32,
    ).astype(jnp.bfloat16)
    info = info.reshape(owner_total, GROUP, LANE)

    outgoing = form_payload(prof, starts, slot_index, coef, info, slot_total)
    incoming = lax.all_to_all(
        outgoing.reshape(owner_total, per_owner, GROUP, LANE), axes, 0, 0, tiled=True
    )
    data = incoming[:, :capacity]
    row_table = incoming[:, capacity].reshape(owner_total, GROUP * LANE)[
        :, : capacity * out_rows
    ].reshape(owner_total, capacity, out_rows)
    gathered = jnp.einsum(
        "dkr,dkql->rql", row_table, data, preferred_element_type=jnp.float32
    )
    gathered = gathered.reshape(out_rows, planes, -1)
    fine = jnp.einsum(
        "rm,mps->rps", interp_weight, prior, preferred_element_type=jnp.float32
    )
    return fine + gathered


def solution(mesh):
    placed = (
        P("pulse", None, "range"),
        P(),
        P("range", "pulse", None),
        P("range", "pulse"),
        P("range", "pulse", None),
        P("range", "pulse"),
        P("range", "pulse"),
        P("range", "pulse"),
        P("pulse", None, "range"),
        P(),
    )
    return jax.shard_map(
        on_device, mesh=mesh, in_specs=placed, out_specs=P("pulse", None, "range"), check_vma=False
    )
```

profile of v0, /device:TPU:1, one launch (start us, length us, event | category | flops | bytes accessed | tf_op | source)
XLA Modules:
  0.0 39.7 jit_solution(15938187985289027541)
XLA Ops:
  0.0 2.1 %collective-permute-start = (bf16[2,2,16384]{2,1,0:T(2,128)(2,1)}, bf16[2,2,16384]{2,1,0:T(2,128)(2,1)S(1)}, u32[]{:S(2)}, u32[]{:S(2)}) collective-permute-start(bf16[2,2,16384]{2,1,0:T(2,128)(2,1)} %param.10), channel_id=1, source_target_pairs={{0,1},{1,0},{2,3},{3,2},{4,5},{5,4},{6,7},{7,6},{8,9},{9,8},{10,11... | collective-permute-start | bytes 393224 | tf_op jit(solution)/shard_map/ppermute | solution.py:133
  2.1 0.7 %sine_multiply_fusion = f32[256]{0:T(256)S(1)} fusion(f32[256]{0:T(256)} %param.11), kind=kLoop, calls=%fused_computation.34 | loop fusion | flops 256 | bytes 2048 | tf_op jit(solution)/shard_map/mul | solution.py:17
  2.8 0.7 %cosine_multiply_fusion = bf16[256]{0:T(256)(128)(2,1)S(1)} fusion(f32[256]{0:T(256)} %param.11), kind=kLoop, calls=%fused_computation.35 | loop fusion | flops 512 | bytes 1536 | tf_op jit(solution)/shard_map/mul | solution.py:16
  3.5 0.7 %reduce-precision_bitcast_fusion = (f32[128,2]{0,1:T(2,128)S(1)}, f32[128,2]{0,1:T(2,128)S(1)}) fusion(f32[1,128,2]{1,2,0:T(2,128)} %param.12), kind=kLoop, calls=%fused_computation.36 | loop fusion | flops 512 | bytes 3072 | tf_op jit(solution)/shard_map/reduce_precision | solution.py:150
  4.9 0.5 %tile.21 = f32[131328]{0:T(1024)S(1)} reshape(f32[256,513]{1,0:T(8,128)S(1)} %tile.20) | data formatting | bytes 1050624 | tf_op jit(solution)/shard_map/tile | solution.py:22
  5.5 0.1 reshape.51
  5.7 0.0 copy-start.3
  5.7 0.6 %tile.9 = bf16[131328]{0:T(1024)(128)(2,1)S(1)} reshape(bf16[256,513]{1,0:T(8,128)(2,1)S(1)} %tile.8) | data formatting | bytes 525312 | tf_op jit(solution)/shard_map/tile | solution.py:22
  6.3 0.2 reshape.50
  6.5 0.1 fusion.13
  6.6 0.2 reduce_window_sum.11
  6.8 0.2 select_reduce_fusion
  7.0 0.5 %bitcast_add_fusion = (s32[128]{0:T(128)S(1)}, s32[128]{0:T(128)}) fusion(s32[1,128]{1,0:T(1,128)S(1)} %copy-done.4, s32[128]{0:T(128)S(1)} %select_reduce_fusion, s32[1,128,1]{1,2,0:T(1,128)S(1)} %copy-done.3), kind=kLoop, calls=%fused_computation.39 | loop fusion | flops 768 | bytes 2560 | tf_op jit(solution)/shard_map/add | solution.py:158
  7.5 0.3 fusion.1
  7.8 0.7 %copy.20 = bf16[4,8,8,128]{3,2,1,0:T(8,128)(2,1)} copy(bf16[4,8,8,128]{3,1,2,0:T(8,128)(2,1)S(1)} %fusion.1) | data formatting | bytes 131072
  8.5 0.6 %stack.4.coef_ref = f32[5,128]{1,0:T(8,128)} concatenate(f32[1,128]{1,0:T(1,128)S(1)} %get-tuple-element.16, f32[1,128]{1,0:T(1,128)S(1)} %get-tuple-element.9, f32[1,128]{1,0:T(1,128)S(1)} %get-tuple-element.17, f32[1,128]{1,0:T(1,128)S(1)} %get-tuple-element.8, f32[1,128]{1,0:T(1,128)S(1)} %fusion.18), dimensions={0} | concatenate | bytes 5120 | tf_op jit(solution)/shard_map/stack | solution.py:151
  9.1 0.4 %broadcast_select_fusion = bf16[2,2,32768]{2,1,0:T(2,128)(2,1)S(1)} fusion(pred[]{:T(512)S(6)} %eq.39, bf16[2,2,16384]{2,1,0:T(2,128)(2,1)S(1)} %collective-permute-done, bf16[2,2,16384]{2,1,0:T(2,128)(2,1)S(1)} %copy-done.1), kind=kLoop, calls=%fused_computation.7 | loop fusion | flops 1179648 | bytes 524289 | tf_op jit(solution)/shard_map/jit(_where)/select_n | solution.py:135
  9.5 0.2 pad.6
  9.7 0.2 reshape.48
  9.9 0.2 fusion.20
  10.1 0.1 maximum_bitcast_fusion
  10.2 0.6 %copy.14 = bf16[2,272,2,384]{3,2,1,0:T(2,128)(2,1)S(1)} copy(bf16[2,272,2,384]{3,1,2,0:T(8,128)(2,1)S(1)} %maximum_bitcast_fusion) | data formatting | bytes 1671168 | tf_op jit(solution)/shard_map/transpose | solution.py:45
  10.9 0.1 copy.19
  11.0 1.2 %convolution_reduce-precision_fusion = f32[544,256]{1,0:T(8,128)} fusion(bf16[544,768]{1,0:T(8,128)(2,1)S(1)} %bitcast.58, bf16[384,128]{0,1:T(8,128)(2,1)S(1)} %slice.74, bf16[384,128]{0,1:T(8,128)(2,1)S(1)} %slice.75, bf16[384,128]{0,1:T(8,128)(2,1)S(1)} %negate_convert_fusion), kind=kOutput, calls=%fused_computation | convolution fusion | flops 215621632 | bytes 1687552 | tf_op jit(solution)/shard_map/dot_general | solution.py:46
  12.2 5.8 %shard_map.100 = bf16[224,8,128]{2,1,0:T(8,128)(2,1)} custom-call(s32[128]{0:T(128)} %bitcast.67, s32[128]{0:T(128)} %get-tuple-element.15.slot_ref, f32[5,128]{1,0:T(8,128)} %stack.4.coef_ref, f32[2,272,256]{2,1,0:T(8,128)} %bitcast.59, bf16[32,8,128]{2,1,0:T(8,128)(2,1)} %bitcast.61), custom_call_target="tpu_custom_call" | custom-call | tf_op jit(solution)/shard_map/pallas_call | solution.py:98
  18.1 5.6 %all-to-all-start = ((bf16[32,7,8,128]{3,2,1,0:T(8,128)(2,1)}), bf16[32,7,8,128]{3,2,1,0:T(8,128)(2,1)S(1)}, u32[]{:S(2)}, u32[]{:S(2)}) async-start(bf16[32,7,8,128]{3,2,1,0:T(8,128)(2,1)} %bitcast.55), calls=%async_computation | async-start | bytes 917504 | tf_op jit(solution)/shard_map/all_to_all | solution.py:167
  23.7 0.2 fusion.11
  23.9 14.3 %all-to-all-done = bf16[32,7,8,128]{3,2,1,0:T(8,128)(2,1)S(1)} async-done(((bf16[32,7,8,128]{3,2,1,0:T(8,128)(2,1)}), bf16[32,7,8,128]{3,2,1,0:T(8,128)(2,1)S(1)}, u32[]{:S(2)}, u32[]{:S(2)}) %all-to-all-start) | async-done | bytes 458784 | tf_op jit(solution)/shard_map/all_to_all | solution.py:167
  38.2 0.2 dot_general.20
  38.4 0.1 reshape.55
  38.5 0.2 fusion
  38.8 0.9 %copy.17 = f32[64,2,512]{2,1,0:T(2,128)} copy(f32[64,2,512]{2,0,1:T(8,128)S(1)} %fusion) | data formatting | bytes 524288 | tf_op jit(solution)/shard_map/add | solution.py:181
  (27 shorter events, 0.3 us)
Async XLA Ops:
  0.0 23.7 %copy-start = (bf16[32,2,512]{2,1,0:T(2,128)(2,1)S(1)}, bf16[32,2,512]{2,1,0:T(2,128)(2,1)}, u32[]{:S(2)}) copy-start(bf16[32,2,512]{2,1,0:T(2,128)(2,1)} %param.18) | copy-start | bytes 196612
  0.0 9.1 %collective-permute-start = (bf16[2,2,16384]{2,1,0:T(2,128)(2,1)}, bf16[2,2,16384]{2,1,0:T(2,128)(2,1)S(1)}, u32[]{:S(2)}, u32[]{:S(2)}) collective-permute-start(bf16[2,2,16384]{2,1,0:T(2,128)(2,1)} %param.10), channel_id=1, source_target_pairs={{0,1},{1,0},{2,3},{3,2},{4,5},{5,4},{6,7},{7,6},{8,9},{9,8},{10,11... | collective-permute-start | bytes 393224 | tf_op jit(solution)/shard_map/ppermute | solution.py:133
  5.7 0.9 %copy-start.3 = (s32[1,128,1]{1,2,0:T(1,128)S(1)}, s32[1,128,1]{1,2,0:T(1,128)}, u32[]{:S(2)}) copy-start(s32[1,128,1]{1,2,0:T(1,128)} %param.14) | copy-start | bytes 1540
  6.3 0.7 %copy-start.4 = (s32[1,128]{1,0:T(1,128)S(1)}, s32[1,128]{1,0:T(1,128)}, u32[]{:S(2)}) copy-start(s32[1,128]{1,0:T(1,128)} %param.15) | copy-start | bytes 1540
  6.3 2.2 %copy-start.5 = (f32[1,128]{1,0:T(1,128)S(1)}, f32[1,128]{1,0:T(1,128)}, u32[]{:S(2)}) copy-start(f32[1,128]{1,0:T(1,128)} %param.16) | copy-start | bytes 1540
  6.3 2.8 %copy-start.1 = (bf16[2,2,16384]{2,1,0:T(2,128)(2,1)S(1)}, bf16[2,2,16384]{2,1,0:T(2,128)(2,1)}, u32[]{:S(2)}) copy-start(bf16[2,2,16384]{2,1,0:T(2,128)(2,1)} %param.10) | copy-start | bytes 393220
  12.2 11.4 %copy-start.2 = (bf16[64,32]{0,1:T(8,128)(2,1)S(1)}, bf16[64,32]{0,1:T(8,128)(2,1)}, u32[]{:S(2)}) copy-start(bf16[64,32]{0,1:T(8,128)(2,1)} %param.19) | copy-start | bytes 12292
  18.1 20.1 %all-to-all-start = ((bf16[32,7,8,128]{3,2,1,0:T(8,128)(2,1)}), bf16[32,7,8,128]{3,2,1,0:T(8,128)(2,1)S(1)}, u32[]{:S(2)}, u32[]{:S(2)}) async-start(bf16[32,7,8,128]{3,2,1,0:T(8,128)(2,1)} %bitcast.55), calls=%async_computation | async-start | bytes 917504 | tf_op jit(solution)/shard_map/all_to_all | solution.py:167
where the time goes:
time: 40 us; the launch traced here: 39.7 us
  waiting for transfers between devices  14.3 us (36%)
  starting transfers between devices  7.64 us (19%)
  Pallas kernels  5.83 us (15%)
  local copies, waits for them, and re-layouts  5.34 us (13%)
  other arithmetic  3.68 us (9%)
  matrix products  1.92 us (5%)
  between operations  0.97 us (2%)
    all_to_all x1, waiting for transfers between devices, on_device(): lax.all_to_all(outgoing.reshape(owner_total, per_owner, GROUP, LANE), axe...  14.3 us
    pallas_call x1, Pallas kernels, form_payload(): pl.pallas_call(records_kernel, out_shape=jax.ShapeDtypeStruct((slot_total...  5.83 us
    all_to_all x1, starting transfers between devices, on_device(): lax.all_to_all(outgoing.reshape(owner_total, per_owner, GROUP, LANE), axe...  5.59 us
    ppermute x1, starting transfers between devices, on_device(): other = lax.ppermute(echo, 'range', [(0, 1), (1, 0)])  2.06 us
    dot_general x1, matrix products, compress_chunks(): jnp.dot(windows, filter_matrix, preferred_element_type=jnp.float32)  1.23 us
    another operation x4, local copies, waits for them, and re-layouts, banded(): jnp.tile(padded, tap_count)[:2 * tap_count * tap_count]  1.18 us
    add x1, local copies, waits for them, and re-layouts, on_device(): return fine + gathered  0.91 us
    unnamed x15, local copies, waits for them, and re-layouts  0.83 us
  transfers between devices with their start and end apart: 2, of which 1 were waited for; matrix products, arithmetic and copies ran while one was open for 16% of the time, Pallas kernels for 0%

commit v1 on v0

--- a/solution.py
+++ b/solution.py
@@ -10,30 +10,38 @@
 GROUP = 8
 
 
+def chirp_kernel(phase_ref, out_ref):
+    taps = phase_ref.shape[1]
+    rows = out_ref.shape[0] // 2
+    span = out_ref.shape[1] // 2
+    phase = phase_ref[...]
+    scale = 1.0 / jnp.sqrt(jnp.float32(taps))
+    bands = []
+    for wave in (jnp.cos(phase) * scale, jnp.sin(phase) * scale):
+        row = jnp.concatenate([wave, jnp.zeros((1, span - taps), jnp.float32)], axis=1)
+        spread = jnp.broadcast_to(row, (rows, span))
+        bands.append(pltpu.roll(spread, 0, 1, stride=1, stride_axis=0))
+    real_band, imag_band = bands
+    out_ref[0:rows, 0:span] = real_band.astype(out_ref.dtype)
+    out_ref[0:rows, span : 2 * span] = imag_band.astype(out_ref.dtype)
+    out_ref[rows : 2 * rows, 0:span] = (-imag_band).astype(out_ref.dtype)
+    out_ref[rows : 2 * rows, span : 2 * span] = real_band.astype(out_ref.dtype)
+
+
 def chirp_matrix(chirp_phase):
-    tap_count = chirp_phase.shape[0]
-    tap_scale = 1.0 / jnp.sqrt(jnp.float32(tap_count))
-    real_taps = jnp.cos(chirp_phase) * tap_scale
-    imag_taps = jnp.sin(chirp_phase) * tap_scale
-
-    def banded(values):
-        padded = jnp.concatenate([values, jnp.zeros((tap_count + 1,), jnp.float32)])
-        return (
-            jnp.tile(padded, tap_count)[: 2 * tap_count * tap_count]
-            .reshape(tap_count, 2 * tap_count)
-            .T
-        )
-
-    real_band = banded(real_taps)[: tap_count + LANE, :LANE]
-    imag_band = banded(imag_taps)[: tap_count + LANE, :LANE]
-    upper = jnp.concatenate([real_band, -imag_band], axis=1)
-    lower = jnp.concatenate([imag_band, real_band], axis=1)
-    return jnp.concatenate([upper, lower], axis=0).astype(jnp.bfloat16)
+    taps = chirp_phase.shape[0]
+    vmem = pl.BlockSpec(memory_space=pltpu.VMEM)
+    return pl.pallas_call(
+        chirp_kernel,
+        out_shape=jax.ShapeDtypeStruct((2 * LANE, 2 * (taps + LANE)), jnp.bfloat16),
+        in_specs=[vmem],
+        out_specs=vmem,
+    )(chirp_phase.reshape(1, taps))
 
 
 def compress_chunks(echo_full, filter_matrix, chunk_total):
     pulses, planes, bin_count = echo_full.shape
-    taps = filter_matrix.shape[0] // planes - LANE
+    taps = filter_matrix.shape[1] // planes - LANE
     reach = taps // LANE
     padded = jnp.pad(
         echo_full, ((0, 0), (0, 0), (0, (chunk_total + reach) * LANE - bin_count))
@@ -43,7 +51,9 @@
         [chunks[:, :, lead : lead + chunk_total] for lead in range(reach + 1)], axis=3
     )
     windows = windows.transpose(0, 2, 1, 3).reshape(pulses * chunk_total, -1)
-    filtered = jnp.dot(windows, filter_matrix, preferred_element_type=jnp.float32)
+    filtered = lax.dot_general(
+        windows, filter_matrix, (((1,), (1,)), ((), ())), preferred_element_type=jnp.float32
+    )
     filtered = lax.reduce_precision(filtered, 8, 7)
     return filtered.reshape(pulses, chunk_total, planes * LANE)
 

time: 40 us -> 42.1 us (1.052)
  Pallas kernels: 5.83 us -> 7.46 us
  local copies, waits for them, and re-layouts: 5.34 us -> 4.67 us
  matrix products: 1.92 us -> 2.58 us
  other arithmetic: 3.68 us -> 4.23 us
    pallas_call x0 -> x1, Pallas kernels: none -> 1.61 us  [chirp_matrix(): pl.pallas_call(chirp_kernel, out_shape=jax.ShapeDtypeStruct((2 * LANE, 2...]
    mul x2 -> x0, other arithmetic: 1.44 us -> none  [the longest x1 0.72 us: chirp_matrix(): real_taps = jnp.cos(chirp_phase) * tap_scale]
    another operation x4 -> x0, local copies, waits for them, and re-layouts: 1.18 us -> none  [banded(): jnp.tile(padded, tap_count)[:2 * tap_count * tap_count]]
    unnamed x15 -> x13, local copies, waits for them, and re-layouts: 0.83 us -> 1.66 us
    add x1, other arithmetic: 0.54 us -> 1.26 us  [on_device(): info_pos = slot_rank * out_rows + dest_rows]
    convert_element_type x1, other arithmetic: 0.08 us -> 0.74 us  [on_device(): (owners[:, None] == jnp.arange(owner_total)[None, :]).astype(jnp.int32)]
    reduce_sum x1, other arithmetic: 0.17 us -> 0.83 us  [on_device(): slot_rank = jnp.sum(earlier * owner_marks, axis=1)]
    dot_general x1, matrix products: 0.26 us -> 0.91 us  [on_device(): jnp.dot(owner_marks.T.astype(jnp.bfloat16), (info_pos[:, None] == jnp.ara...]
  transfers between devices with their start and end apart: 2 -> 2, of which waited for: 1 -> 1; matrix products, arithmetic and copies ran while one was open for 16% -> 15% of each run, Pallas kernels for 0% -> 4%
where the time goes in v1:
time: 42.1 us; the launch traced here: 41.8 us
  waiting for transfers between devices  14.3 us (34%)
  starting transfers between devices  7.71 us (18%)
  Pallas kernels  7.46 us (18%)
  local copies, waits for them, and re-layouts  4.67 us (11%)
  other arithmetic  4.23 us (10%)
  matrix products  2.58 us (6%)
  between operations  0.82 us (2%)
    all_to_all x1, waiting for transfers between devices, on_device(): lax.all_to_all(outgoing.reshape(owner_total, per_owner, GROUP, LANE), axe...  14.3 us
    pallas_call x1, Pallas kernels, form_payload(): pl.pallas_call(records_kernel, out_shape=jax.ShapeDtypeStruct((slot_total...  5.85 us
    all_to_all x1, starting transfers between devices, on_device(): lax.all_to_all(outgoing.reshape(owner_total, per_owner, GROUP, LANE), axe...  5.59 us
    ppermute x1, starting transfers between devices, on_device(): other = lax.ppermute(echo, 'range', [(0, 1), (1, 0)])  2.12 us
    unnamed x13, local copies, waits for them, and re-layouts  1.66 us
    pallas_call x1, Pallas kernels, chirp_matrix(): pl.pallas_call(chirp_kernel, out_shape=jax.ShapeDtypeStruct((2 * LANE, 2...  1.61 us
    add x1, other arithmetic, on_device(): info_pos = slot_rank * out_rows + dest_rows  1.26 us
    dot_general x1, matrix products, compress_chunks(): lax.dot_general(windows, filter_matrix, (((1,), (1,)), ((), ())), preferr...  1.24 us
  transfers between devices with their start and end apart: 2, of which 1 were waited for; matrix products, arithmetic and copies ran while one was open for 15% of the time, Pallas kernels for 4%

profile of v1, /device:TPU:1, one launch (start us, length us, event | category | flops | bytes accessed | tf_op | source)
XLA Modules:
  0.0 41.8 jit_solution(2179318810212044165)
XLA Ops:
  0.0 2.1 %collective-permute-start = (bf16[2,2,16384]{2,1,0:T(2,128)(2,1)}, bf16[2,2,16384]{2,1,0:T(2,128)(2,1)S(1)}, u32[]{:S(2)}, u32[]{:S(2)}) collective-permute-start(bf16[2,2,16384]{2,1,0:T(2,128)(2,1)} %param.10), channel_id=1, source_target_pairs={{0,1},{1,0},{2,3},{3,2},{4,5},{5,4},{6,7},{7,6},{8,9},{9,8},{10,11... | collective-permute-start | bytes 393224 | tf_op jit(solution)/shard_map/ppermute | solution.py:143
  2.1 0.7 %reduce-precision_bitcast_fusion = (f32[128,2]{0,1:T(2,128)S(1)}, f32[128,2]{0,1:T(2,128)S(1)}) fusion(f32[1,128,2]{1,2,0:T(2,128)} %param.12), kind=kLoop, calls=%fused_computation.24 | loop fusion | flops 512 | bytes 3072 | tf_op jit(solution)/shard_map/reduce_precision | solution.py:160
  3.5 0.7 %fusion.6 = s32[128,32]{1,0:T(8,128)S(1)} fusion(s32[128]{0:T(128)} %bitcast.61), kind=kLoop, calls=%fused_computation.16 | loop fusion | flops 8192 | bytes 16896 | tf_op jit(solution)/shard_map/convert_element_type | solution.py:163
  4.3 0.2 reduce_window_sum.11
  4.4 0.8 %select_reduce_fusion = s32[128]{0:T(128)S(1)} fusion(s32[128,32]{1,0:T(8,128)S(1)} %reduce_window_sum.11, s32[128]{0:T(128)} %bitcast.62), kind=kLoop, calls=%fused_computation.14 | loop fusion | flops 20352 | bytes 17408 | tf_op jit(solution)/shard_map/reduce_sum | solution.py:165
  5.3 1.3 %bitcast_add_fusion = (s32[128]{0:T(128)S(1)}, s32[128]{0:T(128)}) fusion(s32[1,128]{1,0:T(1,128)} %param.15, s32[128]{0:T(128)S(1)} %select_reduce_fusion, s32[1,128,1]{1,2,0:T(1,128)} %param.14), kind=kLoop, calls=%fused_computation.27 | loop fusion | flops 768 | bytes 2560 | tf_op jit(solution)/shard_map/add | solution.py:168
  6.5 0.9 %fusion.1 = bf16[4,8,8,128]{3,1,2,0:T(8,128)(2,1)S(1)} fusion(s32[128]{0:T(128)S(1)} %get-tuple-element.14, s32[128]{0:T(128)} %bitcast.63), kind=kOutput, calls=%fused_computation.4 | convolution fusion | flops 8564736 | bytes 66560 | tf_op jit(solution)/shard_map/dot_general | solution.py:169
  7.4 0.6 %copy.20 = bf16[4,8,8,128]{3,2,1,0:T(8,128)(2,1)} copy(bf16[4,8,8,128]{3,1,2,0:T(8,128)(2,1)S(1)} %fusion.1) | data formatting | bytes 131072
  8.1 1.6 %shard_map.100 = bf16[256,768]{1,0:T(8,128)(2,1)} custom-call(f32[1,256]{1,0:T(1,128)} %bitcast.64), custom_call_target="tpu_custom_call" | custom-call | tf_op jit(solution)/shard_map/pallas_call | solution.py:34
  9.7 0.0 copy-done.4
  9.7 0.6 %stack.4.coef_ref = f32[5,128]{1,0:T(8,128)} concatenate(f32[1,128]{1,0:T(1,128)S(1)} %get-tuple-element.16, f32[1,128]{1,0:T(1,128)S(1)} %get-tuple-element.9, f32[1,128]{1,0:T(1,128)S(1)} %get-tuple-element.17, f32[1,128]{1,0:T(1,128)S(1)} %get-tuple-element.8, f32[1,128]{1,0:T(1,128)S(1)} %fusion.11), dimensions={0} | concatenate | bytes 5120 | tf_op jit(solution)/shard_map/stack | solution.py:161
  10.3 0.0 collective-permute-done
  10.3 0.4 broadcast_select_fusion
  10.7 0.2 pad.4
  11.0 0.2 reshape.43
  11.1 0.2 fusion.12
  11.3 0.1 maximum_bitcast_fusion
  11.4 0.6 %copy.14 = bf16[2,272,2,384]{3,2,1,0:T(2,128)(2,1)S(1)} copy(bf16[2,272,2,384]{3,1,2,0:T(8,128)(2,1)S(1)} %maximum_bitcast_fusion) | data formatting | bytes 1671168 | tf_op jit(solution)/shard_map/transpose | solution.py:53
  12.1 0.0 copy-start.1
  12.1 0.1 copy.19
  12.2 0.8 %copy-done.1 = bf16[256,768]{1,0:T(8,128)(2,1)S(1)} copy-done((bf16[256,768]{1,0:T(8,128)(2,1)S(1)}, bf16[256,768]{1,0:T(8,128)(2,1)}, u32[]{:S(2)}) %copy-start.1) | copy-done | bytes 393240
  13.1 1.2 %convolution_reduce-precision_fusion = f32[544,256]{1,0:T(8,128)} fusion(bf16[544,768]{1,0:T(8,128)(2,1)S(1)} %bitcast.54, bf16[256,768]{1,0:T(8,128)(2,1)S(1)} %copy-done.1), kind=kOutput, calls=%fused_computation | convolution fusion | flops 214048768 | bytes 1785856 | tf_op jit(solution)/shard_map/dot_general | solution.py:54
  14.3 5.9 %shard_map.101 = bf16[224,8,128]{2,1,0:T(8,128)(2,1)} custom-call(s32[128]{0:T(128)} %bitcast.65, s32[128]{0:T(128)} %get-tuple-element.15.slot_ref, f32[5,128]{1,0:T(8,128)} %stack.4.coef_ref, f32[2,272,256]{2,1,0:T(8,128)} %bitcast.56, bf16[32,8,128]{2,1,0:T(8,128)(2,1)} %bitcast.58), custom_call_target="tpu_custom_call" | custom-call | tf_op jit(solution)/shard_map/pallas_call | solution.py:108
  20.2 5.6 %all-to-all-start = ((bf16[32,7,8,128]{3,2,1,0:T(8,128)(2,1)}), bf16[32,7,8,128]{3,2,1,0:T(8,128)(2,1)S(1)}, u32[]{:S(2)}, u32[]{:S(2)}) async-start(bf16[32,7,8,128]{3,2,1,0:T(8,128)(2,1)} %bitcast.57), calls=%async_computation | async-start | bytes 917504 | tf_op jit(solution)/shard_map/all_to_all | solution.py:177
  25.8 0.0 copy-done
  25.8 0.0 copy-done.3
  25.8 0.2 fusion.4
  26.0 14.3 %all-to-all-done = bf16[32,7,8,128]{3,2,1,0:T(8,128)(2,1)S(1)} async-done(((bf16[32,7,8,128]{3,2,1,0:T(8,128)(2,1)}), bf16[32,7,8,128]{3,2,1,0:T(8,128)(2,1)S(1)}, u32[]{:S(2)}, u32[]{:S(2)}) %all-to-all-start) | async-done | bytes 458784 | tf_op jit(solution)/shard_map/all_to_all | solution.py:177
  40.3 0.2 dot_general.20
  40.5 0.1 reshape.49
  40.6 0.2 fusion
  40.9 0.9 %copy.17 = f32[64,2,512]{2,1,0:T(2,128)} copy(f32[64,2,512]{2,0,1:T(8,128)S(1)} %fusion) | data formatting | bytes 524288 | tf_op jit(solution)/shard_map/add | solution.py:191
  (11 shorter events, 0.1 us)
Async XLA Ops:
  0.0 25.8 %copy-start = (bf16[32,2,512]{2,1,0:T(2,128)(2,1)S(1)}, bf16[32,2,512]{2,1,0:T(2,128)(2,1)}, u32[]{:S(2)}) copy-start(bf16[32,2,512]{2,1,0:T(2,128)(2,1)} %param.18) | copy-start | bytes 196612
  0.0 10.3 %copy-start.2 = (bf16[2,2,16384]{2,1,0:T(2,128)(2,1)S(1)}, bf16[2,2,16384]{2,1,0:T(2,128)(2,1)}, u32[]{:S(2)}) copy-start(bf16[2,2,16384]{2,1,0:T(2,128)(2,1)} %param.10) | copy-start | bytes 393220
  0.0 9.7 %copy-start.4 = (f32[1,128]{1,0:T(1,128)S(1)}, f32[1,128]{1,0:T(1,128)}, u32[]{:S(2)}) copy-start(f32[1,128]{1,0:T(1,128)} %param.16) | copy-start | bytes 1540
  0.0 10.3 %collective-permute-start = (bf16[2,2,16384]{2,1,0:T(2,128)(2,1)}, bf16[2,2,16384]{2,1,0:T(2,128)(2,1)S(1)}, u32[]{:S(2)}, u32[]{:S(2)}) collective-permute-start(bf16[2,2,16384]{2,1,0:T(2,128)(2,1)} %param.10), channel_id=1, source_target_pairs={{0,1},{1,0},{2,3},{3,2},{4,5},{5,4},{6,7},{7,6},{8,9},{9,8},{10,11... | collective-permute-start | bytes 393224 | tf_op jit(solution)/shard_map/ppermute | solution.py:143
  12.1 1.0 %copy-start.1 = (bf16[256,768]{1,0:T(8,128)(2,1)S(1)}, bf16[256,768]{1,0:T(8,128)(2,1)}, u32[]{:S(2)}) copy-start(bf16[256,768]{1,0:T(8,128)(2,1)} %shard_map.100) | copy-start | bytes 1179652
  14.3 11.5 %copy-start.3 = (bf16[64,32]{0,1:T(8,128)(2,1)S(1)}, bf16[64,32]{0,1:T(8,128)(2,1)}, u32[]{:S(2)}) copy-start(bf16[64,32]{0,1:T(8,128)(2,1)} %param.19) | copy-start | bytes 12292
  20.2 20.1 %all-to-all-start = ((bf16[32,7,8,128]{3,2,1,0:T(8,128)(2,1)}), bf16[32,7,8,128]{3,2,1,0:T(8,128)(2,1)S(1)}, u32[]{:S(2)}, u32[]{:S(2)}) async-start(bf16[32,7,8,128]{3,2,1,0:T(8,128)(2,1)} %bitcast.57), calls=%async_computation | async-start | bytes 917504 | tf_op jit(solution)/shard_map/all_to_all | solution.py:177

commit v2 on v0

--- a/solution.py
+++ b/solution.py
@@ -1,3 +1,5 @@
+import functools
+
 import jax
 import jax.numpy as jnp
 from jax import lax
@@ -48,21 +50,30 @@
     return filtered.reshape(pulses, chunk_total, planes * LANE)
 
 
-def records_kernel(starts_ref, slot_ref, coef_ref, prof_ref, info_ref, out_ref):
+def records_kernel(
+    starts_ref, owner_ref, row_ref, coef_ref, prof_ref, out_ref, counts, *, capacity, out_rows
+):
     slots = starts_ref.shape[0]
-    owners = info_ref.shape[0]
-    per_owner = out_ref.shape[0] // owners
+    owners = counts.shape[0]
+    per_owner = capacity + 1
     lane_ids = lax.broadcasted_iota(jnp.int32, (GROUP, LANE), 1)
     row_ids = lax.broadcasted_iota(jnp.int32, (GROUP, LANE), 0)
+    flat_ids = row_ids * LANE + lane_ids
     out_ref[...] = jnp.zeros(out_ref.shape, out_ref.dtype)
 
-    def put_info(o, carry):
-        out_ref[o * per_owner + per_owner - 1] = info_ref[o]
+    def clear(o, carry):
+        counts[o] = 0
         return carry
 
-    lax.fori_loop(0, owners, put_info, 0)
+    lax.fori_loop(0, owners, clear, 0)
 
     def record(j, carry):
+        owner = jnp.clip(owner_ref[j], 0, owners - 1)
+        rank = jnp.minimum(counts[owner], capacity - 1)
+        counts[owner] = rank + 1
+        info_slot = owner * per_owner + capacity
+        mark = rank * out_rows + jnp.clip(row_ref[j], 0, out_rows - 1)
+        out_ref[info_slot] = jnp.where(flat_ids == mark, 1.0, out_ref[info_slot]).astype(out_ref.dtype)
         st = starts_ref[j]
         first = st // LANE
         off = st - first * LANE
@@ -86,21 +97,25 @@
         tile = jnp.where(
             row_ids < GROUP // 2, shifted[0], pltpu.roll(shifted[1], GROUP // 2, 0)
         )
-        out_ref[slot_ref[j]] = tile.astype(out_ref.dtype)
+        out_ref[owner * per_owner + rank] = tile.astype(out_ref.dtype)
         return carry
 
     lax.fori_loop(0, slots, record, 0, unroll=8)
 
 
-def form_payload(prof, starts, slot_index, coef, info, slot_total):
+def form_payload(prof, starts, owners, dest_rows, coef, owner_total, capacity, out_rows):
     vmem = pl.BlockSpec(memory_space=pltpu.VMEM)
     smem = pl.BlockSpec(memory_space=pltpu.SMEM)
+    kernel = functools.partial(records_kernel, capacity=capacity, out_rows=out_rows)
     return pl.pallas_call(
-        records_kernel,
-        out_shape=jax.ShapeDtypeStruct((slot_total, GROUP, LANE), jnp.bfloat16),
-        in_specs=[smem, smem, smem, vmem, vmem],
+        kernel,
+        out_shape=jax.ShapeDtypeStruct(
+            (owner_total * (capacity + 1), GROUP, LANE), jnp.bfloat16
+        ),
+        in_specs=[smem, smem, smem, smem, vmem],
         out_specs=vmem,
-    )(starts, slot_index, coef, prof, info)
+        scratch_shapes=[pltpu.SMEM((owner_total,), jnp.int32)],
+    )(starts, owners, dest_rows, coef, prof)
 
 
 def on_device(
@@ -146,24 +161,14 @@
     weights = rec_weight[0]
     live_mask = (jnp.arange(slot_count) < rec_count[0, 0]).astype(jnp.float32)
     scales = live_mask * weights / jnp.sqrt(jnp.float32(pulses))
-    cosine = lax.reduce_precision(jnp.cos(phases), 8, 7)
-    sine_part = lax.reduce_precision(jnp.sin(phases), 8, 7)
-    coef = jnp.stack([cosine[:, 0], sine_part[:, 0], cosine[:, 1], sine_part[:, 1], scales])
-
-    owner_marks = (owners[:, None] == jnp.arange(owner_total)[None, :]).astype(jnp.int32)
-    earlier = jnp.cumsum(owner_marks, axis=0) - owner_marks
-    slot_rank = jnp.sum(earlier * owner_marks, axis=1)
-    slot_index = owners * per_owner + jnp.minimum(slot_rank, capacity - 1)
-    slot_index = jnp.clip(slot_index, 0, slot_total - 1).astype(jnp.int32)
-    info_pos = slot_rank * out_rows + dest_rows
-    info = jnp.dot(
-        owner_marks.T.astype(jnp.bfloat16),
-        (info_pos[:, None] == jnp.arange(GROUP * LANE)[None, :]).astype(jnp.bfloat16),
-        preferred_element_type=jnp.float32,
-    ).astype(jnp.bfloat16)
-    info = info.reshape(owner_total, GROUP, LANE)
-
-    outgoing = form_payload(prof, starts, slot_index, coef, info, slot_total)
+    turns = phases.T
+    cosine = lax.reduce_precision(jnp.cos(turns), 8, 7)
+    sine_part = lax.reduce_precision(jnp.sin(turns), 8, 7)
+    coef = jnp.stack([cosine[0], sine_part[0], cosine[1], sine_part[1], scales])
+
+    outgoing = form_payload(
+        prof, starts, owners, dest_rows, coef, owner_total, capacity, out_rows
+    )
     incoming = lax.all_to_all(
         outgoing.reshape(owner_total, per_owner, GROUP, LANE), axes, 0, 0, tiled=True
     )

time: 40 us -> 38.3 us (0.957)
  other arithmetic: 3.68 us -> 2.71 us
  local copies, waits for them, and re-layouts: 5.34 us -> 4.68 us
    unnamed x15 -> x10, local copies, waits for them, and re-layouts: 0.83 us -> 0.17 us
    add x1 -> x0, other arithmetic: 0.54 us -> none  [on_device(): info_pos = slot_rank * out_rows + dest_rows]
  transfers between devices with their start and end apart: 2 -> 2, of which waited for: 1 -> 1; matrix products, arithmetic and copies ran while one was open for 16% -> 12% of each run, Pallas kernels for 0% -> 0%
where the time goes in v2:
time: 38.3 us; the launch traced here: 38 us
  waiting for transfers between devices  14.3 us (37%)
  starting transfers between devices  7.64 us (20%)
  Pallas kernels  6.09 us (16%)
  local copies, waits for them, and re-layouts  4.68 us (12%)
  other arithmetic  2.71 us (7%)
  matrix products  1.65 us (4%)
  between operations  0.94 us (2%)
    all_to_all x1, waiting for transfers between devices, on_device(): lax.all_to_all(outgoing.reshape(owner_total, per_owner, GROUP, LANE), axe...  14.3 us
    pallas_call x1, Pallas kernels, form_payload(): pl.pallas_call(kernel, out_shape=jax.ShapeDtypeStruct((owner_total * (cap...  6.09 us
    all_to_all x1, starting transfers between devices, on_device(): lax.all_to_all(outgoing.reshape(owner_total, per_owner, GROUP, LANE), axe...  5.59 us
    ppermute x1, starting transfers between devices, on_device(): other = lax.ppermute(echo, 'range', [(0, 1), (1, 0)])  2.06 us
    dot_general x1, matrix products, compress_chunks(): jnp.dot(windows, filter_matrix, preferred_element_type=jnp.float32)  1.22 us
    another operation x4, local copies, waits for them, and re-layouts, banded(): jnp.tile(padded, tap_count)[:2 * tap_count * tap_count]  1.18 us
    add x1, local copies, waits for them, and re-layouts, on_device(): return fine + gathered  0.91 us
  transfers between devices with their start and end apart: 2, of which 1 were waited for; matrix products, arithmetic and copies ran while one was open for 12% of the time, Pallas kernels for 0%

profile of v2, /device:TPU:1, one launch (start us, length us, event | category | flops | bytes accessed | tf_op | source)
XLA Modules:
  0.0 38.0 jit_solution(5066632703808974994)
XLA Ops:
  0.0 0.0 copy-start
  0.0 2.1 %collective-permute-start = (bf16[2,2,16384]{2,1,0:T(2,128)(2,1)}, bf16[2,2,16384]{2,1,0:T(2,128)(2,1)S(1)}, u32[]{:S(2)}, u32[]{:S(2)}) collective-permute-start(bf16[2,2,16384]{2,1,0:T(2,128)(2,1)} %param.10), channel_id=1, source_target_pairs={{0,1},{1,0},{2,3},{3,2},{4,5},{5,4},{6,7},{7,6},{8,9},{9,8},{10,11... | collective-permute-start | bytes 393224 | tf_op jit(solution)/shard_map/ppermute | solution.py:148
  2.1 0.7 %sine_multiply_fusion = f32[256]{0:T(256)S(1)} fusion(f32[256]{0:T(256)} %param.11), kind=kLoop, calls=%fused_computation.24 | loop fusion | flops 256 | bytes 2048 | tf_op jit(solution)/shard_map/mul | solution.py:19
  2.8 0.7 %cosine_multiply_fusion = bf16[256]{0:T(256)(128)(2,1)S(1)} fusion(f32[256]{0:T(256)} %param.11), kind=kLoop, calls=%fused_computation.25 | loop fusion | flops 512 | bytes 1536 | tf_op jit(solution)/shard_map/mul | solution.py:18
  3.5 0.7 %reduce-precision_bitcast_fusion = (f32[2,128]{1,0:T(2,128)S(1)}, f32[2,128]{1,0:T(2,128)S(1)}) fusion(f32[1,128,2]{1,2,0:T(2,128)} %param.12), kind=kLoop, calls=%fused_computation.26 | loop fusion | flops 512 | bytes 3072 | tf_op jit(solution)/shard_map/reduce_precision | solution.py:166
  4.9 0.5 %tile.21 = f32[131328]{0:T(1024)S(1)} reshape(f32[256,513]{1,0:T(8,128)S(1)} %tile.20) | data formatting | bytes 1050624 | tf_op jit(solution)/shard_map/tile | solution.py:24
  5.5 0.1 reshape.39
  5.7 0.0 copy-start.3
  5.7 0.6 %tile.9 = bf16[131328]{0:T(1024)(128)(2,1)S(1)} reshape(bf16[256,513]{1,0:T(8,128)(2,1)S(1)} %tile.8) | data formatting | bytes 525312 | tf_op jit(solution)/shard_map/tile | solution.py:24
  6.3 0.0 copy-start.1
  6.3 0.2 reshape.38
  6.5 0.0 copy-done.3
  6.5 0.6 %stack.4.coef_ref = f32[5,128]{1,0:T(8,128)} concatenate(f32[1,128]{1,0:T(1,128)S(1)} %get-tuple-element.14, f32[1,128]{1,0:T(1,128)S(1)} %get-tuple-element.9, f32[1,128]{1,0:T(1,128)S(1)} %get-tuple-element.15, f32[1,128]{1,0:T(1,128)S(1)} %get-tuple-element.8, f32[1,128]{1,0:T(1,128)S(1)} %fusion.14), dimensions={0} | concatenate | bytes 5120 | tf_op jit(solution)/shard_map/stack | solution.py:167
  7.2 0.0 collective-permute-done
  7.2 0.0 copy-done.1
  7.2 0.4 %broadcast_select_fusion = bf16[2,2,32768]{2,1,0:T(2,128)(2,1)S(1)} fusion(pred[]{:T(512)S(6)} %eq.3, bf16[2,2,16384]{2,1,0:T(2,128)(2,1)S(1)} %collective-permute-done, bf16[2,2,16384]{2,1,0:T(2,128)(2,1)S(1)} %copy-done.1), kind=kLoop, calls=%fused_computation.4 | loop fusion | flops 1179648 | bytes 524289 | tf_op jit(solution)/shard_map/jit(_where)/select_n | solution.py:150
  7.6 0.2 pad.6
  7.8 0.2 reshape.36
  8.0 0.2 fusion.16
  8.2 0.1 maximum_bitcast_fusion
  8.3 0.6 %copy.14 = bf16[2,272,2,384]{3,2,1,0:T(2,128)(2,1)S(1)} copy(bf16[2,272,2,384]{3,1,2,0:T(8,128)(2,1)S(1)} %maximum_bitcast_fusion) | data formatting | bytes 1671168 | tf_op jit(solution)/shard_map/transpose | solution.py:47
  9.0 0.1 copy.19
  9.1 1.2 %convolution_reduce-precision_fusion = f32[544,256]{1,0:T(8,128)} fusion(bf16[544,768]{1,0:T(8,128)(2,1)S(1)} %bitcast.49, bf16[384,128]{0,1:T(8,128)(2,1)S(1)} %slice.70, bf16[384,128]{0,1:T(8,128)(2,1)S(1)} %slice.71, bf16[384,128]{0,1:T(8,128)(2,1)S(1)} %negate_convert_fusion), kind=kOutput, calls=%fused_computation | convolution fusion | flops 215621632 | bytes 1687552 | tf_op jit(solution)/shard_map/dot_general | solution.py:48
  10.3 6.1 %shard_map.100 = bf16[224,8,128]{2,1,0:T(8,128)(2,1)} custom-call(s32[128]{0:T(128)} %bitcast.54, s32[128]{0:T(128)} %bitcast.55, s32[128]{0:T(128)} %bitcast.56, f32[5,128]{1,0:T(8,128)} %stack.4.coef_ref, f32[2,272,256]{2,1,0:T(8,128)} %bitcast.50), custom_call_target="tpu_custom_call" | custom-call | tf_op jit(solution)/shard_map/pallas_call | solution.py:110
  16.4 5.6 %all-to-all-start = ((bf16[32,7,8,128]{3,2,1,0:T(8,128)(2,1)}), bf16[32,7,8,128]{3,2,1,0:T(8,128)(2,1)S(1)}, u32[]{:S(2)}, u32[]{:S(2)}) async-start(bf16[32,7,8,128]{3,2,1,0:T(8,128)(2,1)} %bitcast.46), calls=%async_computation | async-start | bytes 917504 | tf_op jit(solution)/shard_map/all_to_all | solution.py:172
  22.0 0.0 copy-done
  22.0 0.2 fusion.9
  22.2 14.3 %all-to-all-done = bf16[32,7,8,128]{3,2,1,0:T(8,128)(2,1)S(1)} async-done(((bf16[32,7,8,128]{3,2,1,0:T(8,128)(2,1)}), bf16[32,7,8,128]{3,2,1,0:T(8,128)(2,1)S(1)}, u32[]{:S(2)}, u32[]{:S(2)}) %all-to-all-start) | async-done | bytes 458784 | tf_op jit(solution)/shard_map/all_to_all | solution.py:172
  36.5 0.2 dot_general.16
  36.7 0.1 reshape.42
  36.9 0.2 fusion
  37.1 0.9 %copy.17 = f32[64,2,512]{2,1,0:T(2,128)} copy(f32[64,2,512]{2,0,1:T(8,128)S(1)} %fusion) | data formatting | bytes 524288 | tf_op jit(solution)/shard_map/add | solution.py:186
  (17 shorter events, 0.2 us)
Async XLA Ops:
  0.0 22.0 %copy-start = (bf16[32,2,512]{2,1,0:T(2,128)(2,1)S(1)}, bf16[32,2,512]{2,1,0:T(2,128)(2,1)}, u32[]{:S(2)}) copy-start(bf16[32,2,512]{2,1,0:T(2,128)(2,1)} %param.18) | copy-start | bytes 196612
  0.0 7.2 %collective-permute-start = (bf16[2,2,16384]{2,1,0:T(2,128)(2,1)}, bf16[2,2,16384]{2,1,0:T(2,128)(2,1)S(1)}, u32[]{:S(2)}, u32[]{:S(2)}) collective-permute-start(bf16[2,2,16384]{2,1,0:T(2,128)(2,1)} %param.10), channel_id=1, source_target_pairs={{0,1},{1,0},{2,3},{3,2},{4,5},{5,4},{6,7},{7,6},{8,9},{9,8},{10,11... | collective-permute-start | bytes 393224 | tf_op jit(solution)/shard_map/ppermute | solution.py:148
  5.7 0.9 %copy-start.3 = (f32[1,128]{1,0:T(1,128)S(1)}, f32[1,128]{1,0:T(1,128)}, u32[]{:S(2)}) copy-start(f32[1,128]{1,0:T(1,128)} %param.16) | copy-start | bytes 1540
  6.3 0.9 %copy-start.1 = (bf16[2,2,16384]{2,1,0:T(2,128)(2,1)S(1)}, bf16[2,2,16384]{2,1,0:T(2,128)(2,1)}, u32[]{:S(2)}) copy-start(bf16[2,2,16384]{2,1,0:T(2,128)(2,1)} %param.10) | copy-start | bytes 393220
  10.3 11.7 %copy-start.2 = (bf16[64,32]{0,1:T(8,128)(2,1)S(1)}, bf16[64,32]{0,1:T(8,128)(2,1)}, u32[]{:S(2)}) copy-start(bf16[64,32]{0,1:T(8,128)(2,1)} %param.19) | copy-start | bytes 12292
  16.4 20.1 %all-to-all-start = ((bf16[32,7,8,128]{3,2,1,0:T(8,128)(2,1)}), bf16[32,7,8,128]{3,2,1,0:T(8,128)(2,1)S(1)}, u32[]{:S(2)}, u32[]{:S(2)}) async-start(bf16[32,7,8,128]{3,2,1,0:T(8,128)(2,1)} %bitcast.46), calls=%async_computation | async-start | bytes 917504 | tf_op jit(solution)/shard_map/all_to_all | solution.py:172

commit v3 on v2

--- a/solution.py
+++ b/solution.py
@@ -51,8 +51,20 @@
 
 
 def records_kernel(
-    starts_ref, owner_ref, row_ref, coef_ref, prof_ref, out_ref, counts, *, capacity, out_rows
+    starts_ref, owner_ref, row_ref, coef_ref, echo_ref, filter_ref, out_ref, counts, prof_ref,
+    *, capacity, out_rows
 ):
+    pulses, planes, _, _ = echo_ref.shape
+    chunk_total = prof_ref.shape[1]
+    reach = filter_ref.shape[0] // (planes * LANE)
+    for k in range(pulses):
+        acc = jnp.zeros((chunk_total, planes * LANE), jnp.float32)
+        for p in range(planes):
+            for lead in range(reach):
+                piece = echo_ref[k, p, lead : lead + chunk_total, :]
+                band = filter_ref[(p * reach + lead) * LANE : (p * reach + lead + 1) * LANE, :]
+                acc = acc + jnp.dot(piece, band, preferred_element_type=jnp.float32)
+        prof_ref[k] = acc.astype(jnp.bfloat16).astype(jnp.float32)
     slots = starts_ref.shape[0]
     owners = counts.shape[0]
     per_owner = capacity + 1
@@ -103,7 +115,7 @@
     lax.fori_loop(0, slots, record, 0, unroll=8)
 
 
-def form_payload(prof, starts, owners, dest_rows, coef, owner_total, capacity, out_rows):
+def form_payload(echo_chunks, filter_matrix, chunk_total, starts, owners, dest_rows, coef, owner_total, capacity, out_rows):
     vmem = pl.BlockSpec(memory_space=pltpu.VMEM)
     smem = pl.BlockSpec(memory_space=pltpu.SMEM)
     kernel = functools.partial(records_kernel, capacity=capacity, out_rows=out_rows)
@@ -112,10 +124,13 @@
         out_shape=jax.ShapeDtypeStruct(
             (owner_total * (capacity + 1), GROUP, LANE), jnp.bfloat16
         ),
-        in_specs=[smem, smem, smem, smem, vmem],
+        in_specs=[smem, smem, smem, smem, vmem, vmem],
         out_specs=vmem,
-        scratch_shapes=[pltpu.SMEM((owner_total,), jnp.int32)],
-    )(starts, owners, dest_rows, coef, prof)
+        scratch_shapes=[
+            pltpu.SMEM((owner_total,), jnp.int32),
+            pltpu.VMEM((echo_chunks.shape[0], chunk_total, 2 * LANE), jnp.float32),
+        ],
+    )(starts, owners, dest_rows, coef, echo_chunks, filter_matrix)
 
 
 def on_device(
@@ -154,7 +169,10 @@
         raw_echo = lax.all_gather(echo, "range", axis=2, tiled=True)
     pulses, planes, bin_total = raw_echo.shape
     chunk_total = bin_total // LANE + 2 * GROUP
-    prof = compress_chunks(raw_echo, filter_matrix, chunk_total)
+    reach = filter_matrix.shape[0] // (planes * LANE)
+    echo_chunks = jnp.pad(
+        raw_echo, ((0, 0), (0, 0), (0, (chunk_total + reach) * LANE - bin_total))
+    ).reshape(pulses, planes, chunk_total + reach, LANE)
 
     starts = rec_start[0]
     phases = rec_phase[0]
@@ -167,7 +185,8 @@
     coef = jnp.stack([cosine[0], sine_part[0], cosine[1], sine_part[1], scales])
 
     outgoing = form_payload(
-        prof, starts, owners, dest_rows, coef, owner_total, capacity, out_rows
+        echo_chunks, filter_matrix, chunk_total, starts, owners, dest_rows, coef,
+        owner_total, capacity, out_rows,
     )
     incoming = lax.all_to_all(
         outgoing.reshape(owner_total, per_owner, GROUP, LANE), axes, 0, 0, tiled=True

time: 38.3 us -> 38.7 us (1.010)
  local copies, waits for them, and re-layouts: 4.68 us -> 6.47 us
  matrix products: 1.65 us -> 0.43 us
  other arithmetic: 2.71 us -> 2.04 us
  Pallas kernels: 6.09 us -> 6.69 us
    unnamed x10 -> x13, local copies, waits for them, and re-layouts: 0.17 us -> 1.4 us
    dot_general x1 -> x0, matrix products: 1.22 us -> none  [compress_chunks(): jnp.dot(windows, filter_matrix, preferred_element_type=jnp.float32)]
    reshape x1, local copies, waits for them, and re-layouts: 0.18 us -> 1.2 us  [on_device(): echo_chunks = jnp.pad(raw_echo, ((0, 0), (0, 0), (0, (chunk_total + reach...]
    concatenate x0 -> x1, other arithmetic: none -> 0.8 us  [chirp_matrix(): return jnp.concatenate([upper, lower], axis=0).astype(jnp.bfloat16)]
    reduce_precision x1, other arithmetic: 0.72 us -> 0.04 us  [on_device(): sine_part = lax.reduce_precision(jnp.sin(turns), 8, 7)]
    mul x1, other arithmetic: 0.72 us -> 0.04 us  [chirp_matrix(): real_taps = jnp.cos(chirp_phase) * tap_scale]
    transpose x1 -> x0, local copies, waits for them, and re-layouts: 0.65 us -> none  [compress_chunks(): windows = windows.transpose(0, 2, 1, 3).reshape(pulses * chunk_total, -1)]
    pallas_call x1, Pallas kernels: 6.09 us -> 6.69 us  [form_payload(): pl.pallas_call(kernel, out_shape=jax.ShapeDtypeStruct((owner_total * (cap...]
  transfers between devices with their start and end apart: 2 -> 2, of which waited for: 1 -> 1; matrix products, arithmetic and copies ran while one was open for 12% -> 11% of each run, Pallas kernels for 0% -> 0%
where the time goes in v3:
time: 38.7 us; the launch traced here: 38.4 us
  waiting for transfers between devices  14.3 us (37%)
  starting transfers between devices  7.65 us (20%)
  Pallas kernels  6.69 us (17%)
  local copies, waits for them, and re-layouts  6.47 us (17%)
  other arithmetic  2.04 us (5%)
  between operations  0.89 us (2%)
  matrix products  0.43 us (1%)
    all_to_all x1, waiting for transfers between devices, on_device(): lax.all_to_all(outgoing.reshape(owner_total, per_owner, GROUP, LANE), axe...  14.3 us
    pallas_call x1, Pallas kernels, form_payload(): pl.pallas_call(kernel, out_shape=jax.ShapeDtypeStruct((owner_total * (cap...  6.69 us
    all_to_all x1, starting transfers between devices, on_device(): lax.all_to_all(outgoing.reshape(owner_total, per_owner, GROUP, LANE), axe...  5.59 us
    ppermute x1, starting transfers between devices, on_device(): other = lax.ppermute(echo, 'range', [(0, 1), (1, 0)])  2.06 us
    unnamed x13, local copies, waits for them, and re-layouts  1.4 us
    reshape x1, local copies, waits for them, and re-layouts, on_device(): echo_chunks = jnp.pad(raw_echo, ((0, 0), (0, 0), (0, (chunk_total + reach...  1.2 us
    another operation x4, local copies, waits for them, and re-layouts, banded(): jnp.tile(padded, tap_count)[:2 * tap_count * tap_count]  1.18 us
    add x1, local copies, waits for them, and re-layouts, on_device(): return fine + gathered  0.91 us
  transfers between devices with their start and end apart: 2, of which 1 were waited for; matrix products, arithmetic and copies ran while one was open for 11% of the time, Pallas kernels for 0%

profile of v3, /device:TPU:1, one launch (start us, length us, event | category | flops | bytes accessed | tf_op | source)
XLA Modules:
  0.0 38.4 jit_solution(559466170302558567)
XLA Ops:
  0.0 0.0 copy-start
  0.0 0.0 copy-start.4
  0.0 2.1 %collective-permute-start = (bf16[2,2,16384]{2,1,0:T(2,128)(2,1)}, bf16[2,2,16384]{2,1,0:T(2,128)(2,1)S(1)}, u32[]{:S(2)}, u32[]{:S(2)}) collective-permute-start(bf16[2,2,16384]{2,1,0:T(2,128)(2,1)} %param.10), channel_id=1, source_target_pairs={{0,1},{1,0},{2,3},{3,2},{4,5},{5,4},{6,7},{7,6},{8,9},{9,8},{10,11... | collective-permute-start | bytes 393224 | tf_op jit(solution)/shard_map/ppermute | solution.py:163
  2.1 0.7 %sine_multiply_fusion = f32[256]{0:T(256)S(1)} fusion(f32[256]{0:T(256)} %param.11), kind=kLoop, calls=%fused_computation.16 | loop fusion | flops 256 | bytes 2048 | tf_op jit(solution)/shard_map/mul | solution.py:19
  2.8 0.0 copy-done.4
  2.8 0.0 copy-start.3
  2.8 0.6 %copy-done.3 = f32[1,128,2]{1,2,0:T(2,128)S(1)} copy-done((f32[1,128,2]{1,2,0:T(2,128)S(1)}, f32[1,128,2]{1,2,0:T(2,128)}, u32[]{:S(2)}) %copy-start.3) | copy-done | bytes 1048
  4.2 0.5 %tile.21 = f32[131328]{0:T(1024)S(1)} reshape(f32[256,513]{1,0:T(8,128)S(1)} %tile.20) | data formatting | bytes 1050624 | tf_op jit(solution)/shard_map/tile | solution.py:24
  4.8 0.1 reshape.32
  4.9 0.2 copy.15
  5.1 0.0 copy-start.5
  5.1 0.6 %copy-done.5 = f32[1,128]{1,0:T(1,128)S(1)} copy-done((f32[1,128]{1,0:T(1,128)S(1)}, f32[1,128]{1,0:T(1,128)}, u32[]{:S(2)}) %copy-start.5) | copy-done | bytes 536
  5.9 0.6 %tile.9 = bf16[131328]{0:T(1024)(128)(2,1)S(1)} reshape(bf16[256,513]{1,0:T(8,128)(2,1)S(1)} %tile.8) | data formatting | bytes 525312 | tf_op jit(solution)/shard_map/tile | solution.py:24
  6.5 0.2 reshape.31
  6.7 0.1 copy.14
  6.8 0.6 %stack.4.coef_ref = f32[5,128]{1,0:T(8,128)} concatenate(f32[1,128]{1,0:T(1,128)S(1)} %get-tuple-element.11, f32[1,128]{1,0:T(1,128)S(1)} %get-tuple-element.6, f32[1,128]{1,0:T(1,128)S(1)} %get-tuple-element.12, f32[1,128]{1,0:T(1,128)S(1)} %get-tuple-element.5, f32[1,128]{1,0:T(1,128)S(1)} %fusion.7), dimensions={0} | concatenate | bytes 5120 | tf_op jit(solution)/shard_map/stack | solution.py:185
  7.4 0.8 %maximum_maximum_fusion.filter_ref = bf16[768,256]{1,0:T(8,128)(2,1)} fusion(bf16[384,128]{1,0:T(8,128)(2,1)S(1)} %slice.55, bf16[384,128]{1,0:T(8,128)(2,1)S(1)} %slice.56, bf16[384,128]{1,0:T(8,128)(2,1)S(1)} %negate_convert_fusion), kind=kLoop, calls=%fused_computation.4 | loop fusion | flops 1572864 | bytes 688128 | tf_op jit(solution)/shard_map/concatenate | solution.py:33
  8.2 0.0 collective-permute-done
  8.2 0.1 copy-done.1
  8.3 0.4 %broadcast_select_fusion = bf16[2,2,32768]{2,1,0:T(2,128)(2,1)S(1)} fusion(pred[]{:T(512)S(6)} %eq.3, bf16[2,2,16384]{2,1,0:T(2,128)(2,1)S(1)} %collective-permute-done, bf16[2,2,16384]{2,1,0:T(2,128)(2,1)S(1)} %copy-done.1), kind=kLoop, calls=%fused_computation.2 | loop fusion | flops 1179648 | bytes 524289 | tf_op jit(solution)/shard_map/jit(_where)/select_n | solution.py:165
  8.7 0.2 pad.6
  9.0 1.2 %reshape.30.echo_ref = bf16[2,2,275,128]{3,2,1,0:T(8,128)(2,1)} reshape(bf16[2,2,35200]{2,1,0:T(2,128)(2,1)S(1)} %pad.6) | data formatting | bytes 563200 | tf_op jit(solution)/shard_map/reshape | solution.py:175
  10.2 6.7 %shard_map.100 = bf16[224,8,128]{2,1,0:T(8,128)(2,1)} custom-call(s32[128]{0:T(128)} %bitcast.44, s32[128]{0:T(128)} %bitcast.45, s32[128]{0:T(128)} %bitcast.46, f32[5,128]{1,0:T(8,128)} %stack.4.coef_ref, bf16[2,2,275,128]{3,2,1,0:T(8,128)(2,1)} %reshape.30.echo_ref, bf16[768,256]{1,0:T(8,128)(2,1)} %maximum_maximum_fusion.filter_ref), custom_call_target="tpu_custom_call" | custom-call | tf_op jit(solution)/shard_map/pallas_call | solution.py:122
  16.8 5.6 %all-to-all-start = ((bf16[32,7,8,128]{3,2,1,0:T(8,128)(2,1)}), bf16[32,7,8,128]{3,2,1,0:T(8,128)(2,1)S(1)}, u32[]{:S(2)}, u32[]{:S(2)}) async-start(bf16[32,7,8,128]{3,2,1,0:T(8,128)(2,1)} %bitcast.38), calls=%async_computation | async-start | bytes 917504 | tf_op jit(solution)/shard_map/all_to_all | solution.py:191
  22.4 0.0 copy-done
  22.5 0.0 copy-done.2
  22.5 0.2 fusion.2
  22.7 14.3 %all-to-all-done = bf16[32,7,8,128]{3,2,1,0:T(8,128)(2,1)S(1)} async-done(((bf16[32,7,8,128]{3,2,1,0:T(8,128)(2,1)}), bf16[32,7,8,128]{3,2,1,0:T(8,128)(2,1)S(1)}, u32[]{:S(2)}, u32[]{:S(2)}) %all-to-all-start) | async-done | bytes 458784 | tf_op jit(solution)/shard_map/all_to_all | solution.py:191
  37.0 0.2 dot_general.12
  37.2 0.1 reshape.34
  37.3 0.2 fusion
  37.5 0.9 %copy.18 = f32[64,2,512]{2,1,0:T(2,128)} copy(f32[64,2,512]{2,0,1:T(8,128)S(1)} %fusion) | data formatting | bytes 524288 | tf_op jit(solution)/shard_map/add | solution.py:205
  (19 shorter events, 0.3 us)
Async XLA Ops:
  0.0 22.4 %copy-start = (bf16[32,2,512]{2,1,0:T(2,128)(2,1)S(1)}, bf16[32,2,512]{2,1,0:T(2,128)(2,1)}, u32[]{:S(2)}) copy-start(bf16[32,2,512]{2,1,0:T(2,128)(2,1)} %param.18) | copy-start | bytes 196612
  0.0 2.8 %copy-start.4 = (f32[256]{0:T(256)S(1)}, f32[256]{0:T(256)}, u32[]{:S(2)}) copy-start(f32[256]{0:T(256)} %param.11) | copy-start | bytes 3076
  0.0 8.2 %collective-permute-start = (bf16[2,2,16384]{2,1,0:T(2,128)(2,1)}, bf16[2,2,16384]{2,1,0:T(2,128)(2,1)S(1)}, u32[]{:S(2)}, u32[]{:S(2)}) collective-permute-start(bf16[2,2,16384]{2,1,0:T(2,128)(2,1)} %param.10), channel_id=1, source_target_pairs={{0,1},{1,0},{2,3},{3,2},{4,5},{5,4},{6,7},{7,6},{8,9},{9,8},{10,11... | collective-permute-start | bytes 393224 | tf_op jit(solution)/shard_map/ppermute | solution.py:163
  2.8 0.7 %copy-start.3 = (f32[1,128,2]{1,2,0:T(2,128)S(1)}, f32[1,128,2]{1,2,0:T(2,128)}, u32[]{:S(2)}) copy-start(f32[1,128,2]{1,2,0:T(2,128)} %param.12) | copy-start | bytes 3076
  5.1 0.7 %copy-start.5 = (f32[1,128]{1,0:T(1,128)S(1)}, f32[1,128]{1,0:T(1,128)}, u32[]{:S(2)}) copy-start(f32[1,128]{1,0:T(1,128)} %param.16) | copy-start | bytes 1540
  7.4 0.9 %copy-start.1 = (bf16[2,2,16384]{2,1,0:T(2,128)(2,1)S(1)}, bf16[2,2,16384]{2,1,0:T(2,128)(2,1)}, u32[]{:S(2)}) copy-start(bf16[2,2,16384]{2,1,0:T(2,128)(2,1)} %param.10) | copy-start | bytes 393220
  16.8 5.6 %copy-start.2 = (bf16[64,32]{0,1:T(8,128)(2,1)S(1)}, bf16[64,32]{0,1:T(8,128)(2,1)}, u32[]{:S(2)}) copy-start(bf16[64,32]{0,1:T(8,128)(2,1)} %param.19) | copy-start | bytes 12292
  16.8 20.1 %all-to-all-start = ((bf16[32,7,8,128]{3,2,1,0:T(8,128)(2,1)}), bf16[32,7,8,128]{3,2,1,0:T(8,128)(2,1)S(1)}, u32[]{:S(2)}, u32[]{:S(2)}) async-start(bf16[32,7,8,128]{3,2,1,0:T(8,128)(2,1)} %bitcast.38), calls=%async_computation | async-start | bytes 917504 | tf_op jit(solution)/shard_map/all_to_all | solution.py:191

commit v4 on v2

--- a/solution.py
+++ b/solution.py
@@ -12,30 +12,51 @@
 GROUP = 8
 
 
-def chirp_matrix(chirp_phase):
-    tap_count = chirp_phase.shape[0]
-    tap_scale = 1.0 / jnp.sqrt(jnp.float32(tap_count))
-    real_taps = jnp.cos(chirp_phase) * tap_scale
-    imag_taps = jnp.sin(chirp_phase) * tap_scale
-
-    def banded(values):
-        padded = jnp.concatenate([values, jnp.zeros((tap_count + 1,), jnp.float32)])
-        return (
-            jnp.tile(padded, tap_count)[: 2 * tap_count * tap_count]
-            .reshape(tap_count, 2 * tap_count)
-            .T
-        )
-
-    real_band = banded(real_taps)[: tap_count + LANE, :LANE]
-    imag_band = banded(imag_taps)[: tap_count + LANE, :LANE]
-    upper = jnp.concatenate([real_band, -imag_band], axis=1)
-    lower = jnp.concatenate([imag_band, real_band], axis=1)
-    return jnp.concatenate([upper, lower], axis=0).astype(jnp.bfloat16)
+def setup_kernel(chirp_ref, turns_ref, scale_ref, filter_ref, coef_ref):
+    taps = chirp_ref.shape[1]
+    rows = filter_ref.shape[0] // 2
+    span = filter_ref.shape[1] // 2
+    phase = chirp_ref[...]
+    tap_scale = 1.0 / jnp.sqrt(jnp.float32(taps))
+    bands = []
+    for wave in (jnp.cos(phase) * tap_scale, jnp.sin(phase) * tap_scale):
+        row = jnp.concatenate([wave, jnp.zeros((1, span - taps), jnp.float32)], axis=1)
+        spread = jnp.broadcast_to(row, (rows, span))
+        bands.append(pltpu.roll(spread, 0, 1, stride=1, stride_axis=0))
+    real_band, imag_band = bands
+    filter_ref[0:rows, 0:span] = real_band.astype(filter_ref.dtype)
+    filter_ref[0:rows, span : 2 * span] = imag_band.astype(filter_ref.dtype)
+    filter_ref[rows : 2 * rows, 0:span] = (-imag_band).astype(filter_ref.dtype)
+    filter_ref[rows : 2 * rows, span : 2 * span] = real_band.astype(filter_ref.dtype)
+    turns = turns_ref[...]
+    cosine = jnp.cos(turns).astype(jnp.bfloat16).astype(jnp.float32)
+    sine_part = jnp.sin(turns).astype(jnp.bfloat16).astype(jnp.float32)
+    coef_ref[...] = jnp.zeros(coef_ref.shape, coef_ref.dtype)
+    coef_ref[0:1, :] = cosine[0:1]
+    coef_ref[1:2, :] = sine_part[0:1]
+    coef_ref[2:3, :] = cosine[1:2]
+    coef_ref[3:4, :] = sine_part[1:2]
+    coef_ref[4:5, :] = scale_ref[...]
+
+
+def setup_tables(chirp_phase, turns, scales):
+    taps = chirp_phase.shape[0]
+    slots = turns.shape[1]
+    vmem = pl.BlockSpec(memory_space=pltpu.VMEM)
+    return pl.pallas_call(
+        setup_kernel,
+        out_shape=(
+            jax.ShapeDtypeStruct((2 * LANE, 2 * (taps + LANE)), jnp.bfloat16),
+            jax.ShapeDtypeStruct((GROUP, slots), jnp.float32),
+        ),
+        in_specs=[vmem, vmem, vmem],
+        out_specs=(vmem, vmem),
+    )(chirp_phase.reshape(1, taps), turns, scales.reshape(1, slots))
 
 
 def compress_chunks(echo_full, filter_matrix, chunk_total):
     pulses, planes, bin_count = echo_full.shape
-    taps = filter_matrix.shape[0] // planes - LANE
+    taps = filter_matrix.shape[1] // planes - LANE
     reach = taps // LANE
     padded = jnp.pad(
         echo_full, ((0, 0), (0, 0), (0, (chunk_total + reach) * LANE - bin_count))
@@ -45,7 +66,9 @@
         [chunks[:, :, lead : lead + chunk_total] for lead in range(reach + 1)], axis=3
     )
     windows = windows.transpose(0, 2, 1, 3).reshape(pulses * chunk_total, -1)
-    filtered = jnp.dot(windows, filter_matrix, preferred_element_type=jnp.float32)
+    filtered = lax.dot_general(
+        windows, filter_matrix, (((1,), (1,)), ((), ())), preferred_element_type=jnp.float32
+    )
     filtered = lax.reduce_precision(filtered, 8, 7)
     return filtered.reshape(pulses, chunk_total, planes * LANE)
 
@@ -143,7 +166,6 @@
     per_owner = capacity + 1
     slot_total = owner_total * per_owner
 
-    filter_matrix = chirp_matrix(chirp_phase)
     if range_count == 2:
         other = lax.ppermute(echo, "range", [(0, 1), (1, 0)])
         first = lax.axis_index("range") == 0
@@ -154,17 +176,14 @@
         raw_echo = lax.all_gather(echo, "range", axis=2, tiled=True)
     pulses, planes, bin_total = raw_echo.shape
     chunk_total = bin_total // LANE + 2 * GROUP
-    prof = compress_chunks(raw_echo, filter_matrix, chunk_total)
 
     starts = rec_start[0]
     phases = rec_phase[0]
     weights = rec_weight[0]
     live_mask = (jnp.arange(slot_count) < rec_count[0, 0]).astype(jnp.float32)
     scales = live_mask * weights / jnp.sqrt(jnp.float32(pulses))
-    turns = phases.T
-    cosine = lax.reduce_precision(jnp.cos(turns), 8, 7)
-    sine_part = lax.reduce_precision(jnp.sin(turns), 8, 7)
-    coef = jnp.stack([cosine[0], sine_part[0], cosine[1], sine_part[1], scales])
+    filter_matrix, coef = setup_tables(chirp_phase, phases.T, scales)
+    prof = compress_chunks(raw_echo, filter_matrix, chunk_total)
 
     outgoing = form_payload(
         prof, starts, owners, dest_rows, coef, owner_total, capacity, out_rows

time: 38.3 us -> 39.9 us (1.042)
  Pallas kernels: 6.09 us -> 7.73 us
  starting transfers between devices: 7.64 us -> 8.98 us
  local copies, waits for them, and re-layouts: 4.68 us -> 3.39 us
    another operation x5 -> x0, local copies, waits for them, and re-layouts: 1.79 us -> none  [the longest x4 1.18 us: banded(): jnp.tile(padded, tap_count)[:2 * tap_count * tap_count]]
    pallas_call x0 -> x1, Pallas kernels: none -> 1.64 us  [setup_tables(): pl.pallas_call(setup_kernel, out_shape=(jax.ShapeDtypeStruct((2 * LANE, 2...]
    mul x2 -> x0, other arithmetic: 1.44 us -> none  [the longest x1 0.72 us: chirp_matrix(): real_taps = jnp.cos(chirp_phase) * tap_scale]
    all_to_all x1, starting transfers between devices: 5.59 us -> 6.93 us  [on_device(): lax.all_to_all(outgoing.reshape(owner_total, per_owner, GROUP, LANE), axe...]
    div x1, other arithmetic: 0.01 us -> 1.25 us  [on_device(): scales = live_mask * weights / jnp.sqrt(jnp.float32(pulses))]
    select_n x1, other arithmetic: 0.41 us -> 1.39 us  [on_device(): jnp.where(first, jnp.concatenate([echo, other], axis=2), jnp.concatenate(...]
    unnamed x10 -> x8, local copies, waits for them, and re-layouts: 0.17 us -> 1.01 us
    reduce_precision x1 -> x0, other arithmetic: 0.72 us -> none  [on_device(): sine_part = lax.reduce_precision(jnp.sin(turns), 8, 7)]
  transfers between devices with their start and end apart: 2 -> 2, of which waited for: 1 -> 1; matrix products, arithmetic and copies ran while one was open for 12% -> 4% of each run, Pallas kernels for 0% -> 4%
where the time goes in v4:
time: 39.9 us; the launch traced here: 39.6 us
  waiting for transfers between devices  14.3 us (36%)
  starting transfers between devices  8.98 us (23%)
  Pallas kernels  7.73 us (19%)
  local copies, waits for them, and re-layouts  3.39 us (8%)
  other arithmetic  2.75 us (7%)
  matrix products  1.65 us (4%)
  between operations  0.79 us (2%)
    all_to_all x1, waiting for transfers between devices, on_device(): lax.all_to_all(outgoing.reshape(owner_total, per_owner, GROUP, LANE), axe...  14.3 us
    all_to_all x1, starting transfers between devices, on_device(): lax.all_to_all(outgoing.reshape(owner_total, per_owner, GROUP, LANE), axe...  6.93 us
    pallas_call x1, Pallas kernels, form_payload(): pl.pallas_call(kernel, out_shape=jax.ShapeDtypeStruct((owner_total * (cap...  6.09 us
    ppermute x1, starting transfers between devices, on_device(): other = lax.ppermute(echo, 'range', [(0, 1), (1, 0)])  2.06 us
    pallas_call x1, Pallas kernels, setup_tables(): pl.pallas_call(setup_kernel, out_shape=(jax.ShapeDtypeStruct((2 * LANE, 2...  1.64 us
    select_n x1, other arithmetic, on_device(): jnp.where(first, jnp.concatenate([echo, other], axis=2), jnp.concatenate(...  1.39 us
    div x1, other arithmetic, on_device(): scales = live_mask * weights / jnp.sqrt(jnp.float32(pulses))  1.25 us
    dot_general x1, matrix products, compress_chunks(): lax.dot_general(windows, filter_matrix, (((1,), (1,)), ((), ())), preferr...  1.22 us
  transfers between devices with their start and end apart: 2, of which 1 were waited for; matrix products, arithmetic and copies ran while one was open for 4% of the time, Pallas kernels for 4%

profile of v4, /device:TPU:1, one launch (start us, length us, event | category | flops | bytes accessed | tf_op | source)
XLA Modules:
  0.0 39.6 jit_solution(5189149931768955646)
XLA Ops:
  0.0 0.0 copy-start
  0.0 2.1 %collective-permute-start = (bf16[2,2,16384]{2,1,0:T(2,128)(2,1)}, bf16[2,2,16384]{2,1,0:T(2,128)(2,1)S(1)}, u32[]{:S(2)}, u32[]{:S(2)}) collective-permute-start(bf16[2,2,16384]{2,1,0:T(2,128)(2,1)} %param.10), channel_id=1, source_target_pairs={{0,1},{1,0},{2,3},{3,2},{4,5},{5,4},{6,7},{7,6},{8,9},{9,8},{10,11... | collective-permute-start | bytes 393224 | tf_op jit(solution)/shard_map/ppermute | solution.py:170
  2.7 1.3 %fusion.7.scale_ref = f32[1,128]{1,0:T(1,128)} fusion(f32[1,128]{1,0:T(1,128)} %param.16, s32[]{:T(128)} %bitcast.39), kind=kLoop, calls=%fused_computation.14 | loop fusion | flops 384 | bytes 1028 | tf_op jit(solution)/shard_map/div | solution.py:184
  4.0 1.6 %shard_map.100 = (bf16[256,768]{1,0:T(8,128)(2,1)}, f32[8,128]{1,0:T(8,128)}) custom-call(f32[1,256]{1,0:T(1,128)} %bitcast.46, f32[2,128]{1,0:T(2,128)} %bitcast.47, f32[1,128]{1,0:T(1,128)} %fusion.7.scale_ref), custom_call_target="tpu_custom_call" | custom-call | tf_op jit(solution)/shard_map/pallas_call | solution.py:46
  5.6 0.0 collective-permute-done
  5.6 1.4 %broadcast_select_fusion = bf16[2,2,32768]{2,1,0:T(2,128)(2,1)S(1)} fusion(pred[]{:T(512)S(6)} %eq.3, bf16[2,2,16384]{2,1,0:T(2,128)(2,1)S(1)} %collective-permute-done, bf16[2,2,16384]{2,1,0:T(2,128)(2,1)} %param.10), kind=kLoop, calls=%fused_computation.4 | loop fusion | flops 1179648 | bytes 524289 | tf_op jit(solution)/shard_map/jit(_where)/select_n | solution.py:172
  7.0 0.2 pad.4
  7.2 0.2 reshape.29
  7.4 0.2 fusion.8
  7.6 0.1 maximum_bitcast_fusion
  7.7 0.6 %copy.14 = bf16[2,272,2,384]{3,2,1,0:T(2,128)(2,1)S(1)} copy(bf16[2,272,2,384]{3,1,2,0:T(8,128)(2,1)S(1)} %maximum_bitcast_fusion) | data formatting | bytes 1671168 | tf_op jit(solution)/shard_map/transpose | solution.py:68
  8.3 0.0 copy-start.1
  8.4 0.1 copy.19
  8.5 0.8 %copy-done.1 = bf16[256,768]{1,0:T(8,128)(2,1)S(1)} copy-done((bf16[256,768]{1,0:T(8,128)(2,1)S(1)}, bf16[256,768]{1,0:T(8,128)(2,1)}, u32[]{:S(2)}) %copy-start.1) | copy-done | bytes 393240
  9.3 1.2 %convolution_reduce-precision_fusion = f32[544,256]{1,0:T(8,128)} fusion(bf16[544,768]{1,0:T(8,128)(2,1)S(1)} %bitcast.40, bf16[256,768]{1,0:T(8,128)(2,1)S(1)} %copy-done.1), kind=kOutput, calls=%fused_computation | convolution fusion | flops 214048768 | bytes 1785856 | tf_op jit(solution)/shard_map/dot_general | solution.py:69
  10.6 0.0 copy-start.2
  10.6 6.1 %shard_map.101 = bf16[224,8,128]{2,1,0:T(8,128)(2,1)} custom-call(s32[128]{0:T(128)} %bitcast.48, s32[128]{0:T(128)} %bitcast.49, s32[128]{0:T(128)} %bitcast.50, f32[8,128]{1,0:T(8,128)} %get-tuple-element.7.coef_ref, f32[2,272,256]{2,1,0:T(8,128)} %bitcast.42), custom_call_target="tpu_custom_call" | custom-call | tf_op jit(solution)/shard_map/pallas_call | solution.py:133
  16.6 6.9 %all-to-all-start = ((bf16[32,7,8,128]{3,2,1,0:T(8,128)(2,1)}), bf16[32,7,8,128]{3,2,1,0:T(8,128)(2,1)S(1)}, u32[]{:S(2)}, u32[]{:S(2)}) async-start(bf16[32,7,8,128]{3,2,1,0:T(8,128)(2,1)} %bitcast.43), calls=%async_computation | async-start | bytes 917504 | tf_op jit(solution)/shard_map/all_to_all | solution.py:191
  23.6 0.0 copy-done
  23.6 0.0 copy-done.2
  23.6 0.2 fusion.2
  23.8 14.3 %all-to-all-done = bf16[32,7,8,128]{3,2,1,0:T(8,128)(2,1)S(1)} async-done(((bf16[32,7,8,128]{3,2,1,0:T(8,128)(2,1)}), bf16[32,7,8,128]{3,2,1,0:T(8,128)(2,1)S(1)}, u32[]{:S(2)}, u32[]{:S(2)}) %all-to-all-start) | async-done | bytes 458784 | tf_op jit(solution)/shard_map/all_to_all | solution.py:191
  38.1 0.2 dot_general.16
  38.3 0.1 reshape.33
  38.4 0.2 fusion
  38.7 0.9 %copy.17 = f32[64,2,512]{2,1,0:T(2,128)} copy(f32[64,2,512]{2,0,1:T(8,128)S(1)} %fusion) | data formatting | bytes 524288 | tf_op jit(solution)/shard_map/add | solution.py:205
  (4 shorter events, 0.0 us)
Async XLA Ops:
  0.0 23.6 %copy-start = (bf16[32,2,512]{2,1,0:T(2,128)(2,1)S(1)}, bf16[32,2,512]{2,1,0:T(2,128)(2,1)}, u32[]{:S(2)}) copy-start(bf16[32,2,512]{2,1,0:T(2,128)(2,1)} %param.18) | copy-start | bytes 196612
  0.0 5.6 %collective-permute-start = (bf16[2,2,16384]{2,1,0:T(2,128)(2,1)}, bf16[2,2,16384]{2,1,0:T(2,128)(2,1)S(1)}, u32[]{:S(2)}, u32[]{:S(2)}) collective-permute-start(bf16[2,2,16384]{2,1,0:T(2,128)(2,1)} %param.10), channel_id=1, source_target_pairs={{0,1},{1,0},{2,3},{3,2},{4,5},{5,4},{6,7},{7,6},{8,9},{9,8},{10,11... | collective-permute-start | bytes 393224 | tf_op jit(solution)/shard_map/ppermute | solution.py:170
  8.3 1.0 %copy-start.1 = (bf16[256,768]{1,0:T(8,128)(2,1)S(1)}, bf16[256,768]{1,0:T(8,128)(2,1)}, u32[]{:S(2)}) copy-start(bf16[256,768]{1,0:T(8,128)(2,1)} %get-tuple-element.8) | copy-start | bytes 1179652
  10.6 13.0 %copy-start.2 = (bf16[64,32]{0,1:T(8,128)(2,1)S(1)}, bf16[64,32]{0,1:T(8,128)(2,1)}, u32[]{:S(2)}) copy-start(bf16[64,32]{0,1:T(8,128)(2,1)} %param.19) | copy-start | bytes 12292
  16.6 21.4 %all-to-all-start = ((bf16[32,7,8,128]{3,2,1,0:T(8,128)(2,1)}), bf16[32,7,8,128]{3,2,1,0:T(8,128)(2,1)S(1)}, u32[]{:S(2)}, u32[]{:S(2)}) async-start(bf16[32,7,8,128]{3,2,1,0:T(8,128)(2,1)} %bitcast.43), calls=%async_computation | async-start | bytes 917504 | tf_op jit(solution)/shard_map/all_to_all | solution.py:191

commit v5 on v2

--- a/solution.py
+++ b/solution.py
@@ -55,10 +55,9 @@
 ):
     slots = starts_ref.shape[0]
     owners = counts.shape[0]
-    per_owner = capacity + 1
+    per_owner = capacity
     lane_ids = lax.broadcasted_iota(jnp.int32, (GROUP, LANE), 1)
     row_ids = lax.broadcasted_iota(jnp.int32, (GROUP, LANE), 0)
-    flat_ids = row_ids * LANE + lane_ids
     out_ref[...] = jnp.zeros(out_ref.shape, out_ref.dtype)
 
     def clear(o, carry):
@@ -71,9 +70,6 @@
         owner = jnp.clip(owner_ref[j], 0, owners - 1)
         rank = jnp.minimum(counts[owner], capacity - 1)
         counts[owner] = rank + 1
-        info_slot = owner * per_owner + capacity
-        mark = rank * out_rows + jnp.clip(row_ref[j], 0, out_rows - 1)
-        out_ref[info_slot] = jnp.where(flat_ids == mark, 1.0, out_ref[info_slot]).astype(out_ref.dtype)
         st = starts_ref[j]
         first = st // LANE
         off = st - first * LANE
@@ -110,7 +106,7 @@
     return pl.pallas_call(
         kernel,
         out_shape=jax.ShapeDtypeStruct(
-            (owner_total * (capacity + 1), GROUP, LANE), jnp.bfloat16
+            (owner_total * capacity, GROUP, LANE), jnp.bfloat16
         ),
         in_specs=[smem, smem, smem, smem, vmem],
         out_specs=vmem,
@@ -140,8 +136,11 @@
     dest_rows = rec_row[0]
     out_rows = interp_weight.shape[0]
     capacity = max(2, 3 * slot_count // (2 * owner_total))
-    per_owner = capacity + 1
-    slot_total = owner_total * per_owner
+    per_owner = capacity
+    codes = (owners * out_rows + dest_rows).astype(jnp.float32)
+    all_codes = lax.all_gather(codes, axes, axis=0, tiled=False)
+    all_codes, echo = lax.optimization_barrier((all_codes, echo))
+    all_codes = all_codes.astype(jnp.int32)
 
     filter_matrix = chirp_matrix(chirp_phase)
     if range_count == 2:
@@ -172,10 +171,16 @@
     incoming = lax.all_to_all(
         outgoing.reshape(owner_total, per_owner, GROUP, LANE), axes, 0, 0, tiled=True
     )
-    data = incoming[:, :capacity]
-    row_table = incoming[:, capacity].reshape(owner_total, GROUP * LANE)[
-        :, : capacity * out_rows
-    ].reshape(owner_total, capacity, out_rows)
+    data = incoming
+    me = lax.axis_index("pulse") * range_count + lax.axis_index("range")
+    mine = (all_codes // out_rows == me).astype(jnp.int32)
+    rank = jnp.cumsum(mine, axis=1) - mine
+    picks = (mine[:, None, :] == 1) & (rank[:, None, :] == jnp.arange(capacity)[None, :, None])
+    slot_rows = jnp.sum(jnp.where(picks, (all_codes % out_rows)[:, None, :], 0), axis=2)
+    taken = jnp.any(picks, axis=2)
+    row_table = (
+        taken[:, :, None] & (slot_rows[:, :, None] == jnp.arange(out_rows)[None, None, :])
+    ).astype(jnp.bfloat16)
     gathered = jnp.einsum(
         "dkr,dkql->rql", row_table, data, preferred_element_type=jnp.float32
     )

time: 38.3 us -> 102 us (2.66)
  blocking collectives: 0 us -> 66.3 us
  waiting for transfers between devices: 14.3 us -> 12.6 us
  starting transfers between devices: 7.64 us -> 6.3 us
    all_gather x0 -> x1, blocking collectives: none -> 66.3 us  [on_device(): all_codes = lax.all_gather(codes, axes, axis=0, tiled=False)]
    ppermute x1, starting transfers between devices: 2.06 us -> 0.01 us  [on_device(): other = lax.ppermute(echo, 'range', [(0, 1), (1, 0)])]
    all_to_all x1, waiting for transfers between devices: 14.3 us -> 12.6 us  [on_device(): lax.all_to_all(outgoing.reshape(owner_total, per_owner, GROUP, LANE), axe...]
  transfers between devices with their start and end apart: 2 -> 2, of which waited for: 1 -> 1; matrix products, arithmetic and copies ran while one was open for 12% -> 4% of each run, Pallas kernels for 0% -> 0%
where the time goes in v5:
time: 102 us
  blocking collectives  66.3 us (65%)
  waiting for transfers between devices  12.6 us (12%)
  starting transfers between devices  6.3 us (6%)
  Pallas kernels  5.86 us (6%)
  local copies, waits for them, and re-layouts  4.68 us (5%)
  other arithmetic  3.43 us (3%)
  matrix products  1.75 us (2%)
    all_gather x1, blocking collectives, on_device(): all_codes = lax.all_gather(codes, axes, axis=0, tiled=False)  66.3 us
    all_to_all x1, waiting for transfers between devices, on_device(): lax.all_to_all(outgoing.reshape(owner_total, per_owner, GROUP, LANE), axe...  12.6 us
    all_to_all x1, starting transfers between devices, on_device(): lax.all_to_all(outgoing.reshape(owner_total, per_owner, GROUP, LANE), axe...  6.3 us
    pallas_call x1, Pallas kernels, form_payload(): pl.pallas_call(kernel, out_shape=jax.ShapeDtypeStruct((owner_total * capa...  5.86 us
  transfers between devices with their start and end apart: 2, of which 1 were waited for; matrix products, arithmetic and copies ran while one was open for 4% of the time, Pallas kernels for 0%

profile of v5, /device:TPU:1, one launch (start us, length us, event | category | flops | bytes accessed | tf_op | source)
XLA Modules:
  0.0 101.9 jit_solution(894945808281695180)
XLA Ops:
  0.0 0.7 fusion.23
  0.7 66.3 %all-gather = f32[32,1,128]{2,1,0:T(1,128)S(1)} all-gather(f32[1,1,128]{2,1,0:T(1,128)S(1)} %fusion.23), channel_id=1, replica_groups=mesh['pulse'=16,'range'=2] {'pulse','range'}, dimensions={0}, use_global_device_ids=true | all-gather | bytes 16896 | tf_op jit(solution)/shard_map/all_gather | solution.py:141
  67.1 0.7 sine_multiply_fusion
  67.8 0.7 cosine_multiply_fusion
  68.6 0.5 tile.21
  69.1 0.1 reshape.55
  69.3 0.0 copy-start.3
  69.3 0.0 copy-start.4
  69.3 0.6 tile.9
  69.9 0.0 copy-start.1
  69.9 0.2 reshape.54
  70.9 0.6 stack.4.coef_ref
  71.5 0.4 broadcast_select_fusion
  72.0 0.2 pad.6
  72.2 0.2 reshape.52
  72.4 0.2 fusion.26
  72.5 0.1 maximum_bitcast_fusion
  72.6 0.6 copy.36
  73.3 0.1 copy.42
  73.4 1.2 %convolution_reduce-precision_fusion = f32[544,256]{1,0:T(8,128)} fusion(bf16[544,768]{1,0:T(8,128)(2,1)S(1)} %bitcast.45, bf16[384,128]{0,1:T(8,128)(2,1)S(1)} %slice.54, bf16[384,128]{0,1:T(8,128)(2,1)S(1)} %slice.55, bf16[384,128]{0,1:T(8,128)(2,1)S(1)} %negate_convert_fusion), kind=kOutput, calls=%fused_computation | convolution fusion | flops 215621632 | bytes 1687552 | tf_op jit(solution)/shard_map/dot_general | solution.py:48
  74.7 5.9 %shard_map.100 = bf16[192,8,128]{2,1,0:T(8,128)(2,1)} custom-call(s32[128]{0:T(128)} %bitcast.50, s32[128]{0:T(128)} %bitcast.51, s32[128]{0:T(128)} %bitcast.52, f32[5,128]{1,0:T(8,128)} %stack.4.coef_ref, f32[2,272,256]{2,1,0:T(8,128)} %bitcast.46), custom_call_target="tpu_custom_call" | custom-call | tf_op jit(solution)/shard_map/pallas_call | solution.py:106
  80.5 6.3 %all-to-all-start = ((bf16[32,6,8,128]{3,2,1,0:T(8,128)(2,1)}), bf16[32,6,8,128]{3,2,1,0:T(8,128)(2,1)S(1)}, u32[]{:S(2)}, u32[]{:S(2)}) async-start(bf16[32,6,8,128]{3,2,1,0:T(8,128)(2,1)} %bitcast.42), calls=%async_computation | async-start | bytes 786432 | tf_op jit(solution)/shard_map/all_to_all | solution.py:171
  86.9 0.3 reduce_window_sum.11
  87.2 0.2 fusion.9
  87.4 0.2 select_reduce_fusion
  87.5 0.0 copy-start.2
  87.6 12.6 %all-to-all-done = bf16[32,6,8,128]{3,2,1,0:T(8,128)(2,1)S(1)} async-done(((bf16[32,6,8,128]{3,2,1,0:T(8,128)(2,1)}), bf16[32,6,8,128]{3,2,1,0:T(8,128)(2,1)S(1)}, u32[]{:S(2)}, u32[]{:S(2)}) %all-to-all-start) | async-done | bytes 393248 | tf_op jit(solution)/shard_map/all_to_all | solution.py:171
  100.1 0.3 convolution_bitcast_fusion
  100.5 0.2 copy.38
  100.6 0.1 reshape.58
  100.8 0.2 convolution_add_fusion
  101.0 0.9 copy.40
  (23 shorter events, 0.3 us)
Async XLA Ops:
  0.0 100.8 %copy-start = (bf16[32,2,512]{2,1,0:T(2,128)(2,1)S(1)}, bf16[32,2,512]{2,1,0:T(2,128)(2,1)}, u32[]{:S(2)}) copy-start(bf16[32,2,512]{2,1,0:T(2,128)(2,1)} %param.18) | copy-start | bytes 196612
  67.1 4.5 %collective-permute-start = (bf16[2,2,16384]{2,1,0:T(2,128)(2,1)}, bf16[2,2,16384]{2,1,0:T(2,128)(2,1)S(1)}, u32[]{:S(2)}, u32[]{:S(2)}) collective-permute-start(bf16[2,2,16384]{2,1,0:T(2,128)(2,1)} %param.10), channel_id=1, source_target_pairs={{0,1},{1,0},{2,3},{3,2},{4,5},{5,4},{6,7},{7,6},{8,9},{9,8},{10,11... | collective-permute-start | bytes 393224 | tf_op jit(solution)/shard_map/ppermute | solution.py:147
  69.3 0.9 copy-start.3
  69.3 1.6 %copy-start.4 = (f32[1,128]{1,0:T(1,128)S(1)}, f32[1,128]{1,0:T(1,128)}, u32[]{:S(2)}) copy-start(f32[1,128]{1,0:T(1,128)} %param.16) | copy-start | bytes 1540
  69.9 1.6 %copy-start.1 = (bf16[2,2,16384]{2,1,0:T(2,128)(2,1)S(1)}, bf16[2,2,16384]{2,1,0:T(2,128)(2,1)}, u32[]{:S(2)}) copy-start(bf16[2,2,16384]{2,1,0:T(2,128)(2,1)} %param.10) | copy-start | bytes 393220
  80.5 19.6 %all-to-all-start = ((bf16[32,6,8,128]{3,2,1,0:T(8,128)(2,1)}), bf16[32,6,8,128]{3,2,1,0:T(8,128)(2,1)S(1)}, u32[]{:S(2)}, u32[]{:S(2)}) async-start(bf16[32,6,8,128]{3,2,1,0:T(8,128)(2,1)} %bitcast.42), calls=%async_computation | async-start | bytes 786432 | tf_op jit(solution)/shard_map/all_to_all | solution.py:171
  87.5 13.2 %copy-start.2 = (bf16[64,32]{0,1:T(8,128)(2,1)S(1)}, bf16[64,32]{0,1:T(8,128)(2,1)}, u32[]{:S(2)}) copy-start(bf16[64,32]{0,1:T(8,128)(2,1)} %param.19) | copy-start | bytes 12292

commit v6 on v2

--- a/solution.py
+++ b/solution.py
@@ -68,17 +68,18 @@
     lax.fori_loop(0, owners, clear, 0)
 
     def record(j, carry):
-        owner = jnp.clip(owner_ref[j], 0, owners - 1)
+        owner = jnp.minimum(owner_ref[j], owners - 1)
         rank = jnp.minimum(counts[owner], capacity - 1)
         counts[owner] = rank + 1
-        info_slot = owner * per_owner + capacity
-        mark = rank * out_rows + jnp.clip(row_ref[j], 0, out_rows - 1)
+        base_slot = owner * per_owner
+        info_slot = base_slot + capacity
+        mark = rank * out_rows + (row_ref[j] & (out_rows - 1))
         out_ref[info_slot] = jnp.where(flat_ids == mark, 1.0, out_ref[info_slot]).astype(out_ref.dtype)
         st = starts_ref[j]
-        first = st // LANE
-        off = st - first * LANE
-        aligned = pl.multiple_of((first // GROUP) * GROUP, GROUP)
-        lift = (2 * GROUP - (first - aligned)) % (2 * GROUP)
+        first = lax.shift_right_logical(st, 7)
+        off = st & (LANE - 1)
+        aligned = pl.multiple_of(first & -GROUP, GROUP)
+        lift = (2 * GROUP - (first & (GROUP - 1))) & (2 * GROUP - 1)
         parts = []
         for k in range(2):
             rows = prof_ref[k, pl.ds(aligned, 2 * GROUP), :]
@@ -88,7 +89,7 @@
         c0, s0, c1, s1, sc = (coef_ref[i, j] for i in range(5))
         out_re = ((c0 * re0 + c1 * re1) - (s0 * im0 + s1 * im1)) * sc
         out_im = ((c0 * im0 + c1 * im1) + (s0 * re0 + s1 * re1)) * sc
-        turn = (LANE - off) % LANE
+        turn = (LANE - off) & (LANE - 1)
         keep = lane_ids < LANE - off
         shifted = []
         for z in (out_re, out_im):
@@ -97,7 +98,7 @@
         tile = jnp.where(
             row_ids < GROUP // 2, shifted[0], pltpu.roll(shifted[1], GROUP // 2, 0)
         )
-        out_ref[owner * per_owner + rank] = tile.astype(out_ref.dtype)
+        out_ref[base_slot + rank] = tile.astype(out_ref.dtype)
         return carry
 
     lax.fori_loop(0, slots, record, 0, unroll=8)

time: 38.3 us -> 36.6 us (0.956)
  Pallas kernels: 6.09 us -> 4.4 us
    pallas_call x1, Pallas kernels: 6.09 us -> 4.4 us  [form_payload(): pl.pallas_call(kernel, out_shape=jax.ShapeDtypeStruct((owner_total * (cap...]
where the time goes in v6:
time: 36.6 us; the launch traced here: 36.3 us
  waiting for transfers between devices  14.3 us (39%)
  starting transfers between devices  7.64 us (21%)
  local copies, waits for them, and re-layouts  4.68 us (13%)
  Pallas kernels  4.4 us (12%)
  other arithmetic  2.71 us (7%)
  matrix products  1.65 us (5%)
  between operations  0.94 us (3%)
    all_to_all x1, waiting for transfers between devices, on_device(): lax.all_to_all(outgoing.reshape(owner_total, per_owner, GROUP, LANE), axe...  14.3 us
    all_to_all x1, starting transfers between devices, on_device(): lax.all_to_all(outgoing.reshape(owner_total, per_owner, GROUP, LANE), axe...  5.59 us
    pallas_call x1, Pallas kernels, form_payload(): pl.pallas_call(kernel, out_shape=jax.ShapeDtypeStruct((owner_total * (cap...  4.4 us
    ppermute x1, starting transfers between devices, on_device(): other = lax.ppermute(echo, 'range', [(0, 1), (1, 0)])  2.06 us
    dot_general x1, matrix products, compress_chunks(): jnp.dot(windows, filter_matrix, preferred_element_type=jnp.float32)  1.22 us
    another operation x4, local copies, waits for them, and re-layouts, banded(): jnp.tile(padded, tap_count)[:2 * tap_count * tap_count]  1.18 us
    add x1, local copies, waits for them, and re-layouts, on_device(): return fine + gathered  0.91 us
  transfers between devices with their start and end apart: 2, of which 1 were waited for; matrix products, arithmetic and copies ran while one was open for 12% of the time, Pallas kernels for 0%

profile of v6, /device:TPU:1, one launch (start us, length us, event | category | flops | bytes accessed | tf_op | source)
XLA Modules:
  0.0 36.3 jit_solution(10661977053013973862)
XLA Ops:
  0.0 0.0 copy-start
  0.0 2.1 %collective-permute-start = (bf16[2,2,16384]{2,1,0:T(2,128)(2,1)}, bf16[2,2,16384]{2,1,0:T(2,128)(2,1)S(1)}, u32[]{:S(2)}, u32[]{:S(2)}) collective-permute-start(bf16[2,2,16384]{2,1,0:T(2,128)(2,1)} %param.10), channel_id=1, source_target_pairs={{0,1},{1,0},{2,3},{3,2},{4,5},{5,4},{6,7},{7,6},{8,9},{9,8},{10,11... | collective-permute-start | bytes 393224 | tf_op jit(solution)/shard_map/ppermute | solution.py:149
  2.1 0.7 %sine_multiply_fusion = f32[256]{0:T(256)S(1)} fusion(f32[256]{0:T(256)} %param.11), kind=kLoop, calls=%fused_computation.24 | loop fusion | flops 256 | bytes 2048 | tf_op jit(solution)/shard_map/mul | solution.py:19
  2.8 0.7 %cosine_multiply_fusion = bf16[256]{0:T(256)(128)(2,1)S(1)} fusion(f32[256]{0:T(256)} %param.11), kind=kLoop, calls=%fused_computation.25 | loop fusion | flops 512 | bytes 1536 | tf_op jit(solution)/shard_map/mul | solution.py:18
  3.5 0.7 %reduce-precision_bitcast_fusion = (f32[2,128]{1,0:T(2,128)S(1)}, f32[2,128]{1,0:T(2,128)S(1)}) fusion(f32[1,128,2]{1,2,0:T(2,128)} %param.12), kind=kLoop, calls=%fused_computation.26 | loop fusion | flops 512 | bytes 3072 | tf_op jit(solution)/shard_map/reduce_precision | solution.py:167
  4.9 0.5 %tile.21 = f32[131328]{0:T(1024)S(1)} reshape(f32[256,513]{1,0:T(8,128)S(1)} %tile.20) | data formatting | bytes 1050624 | tf_op jit(solution)/shard_map/tile | solution.py:24
  5.5 0.1 reshape.39
  5.7 0.0 copy-start.3
  5.7 0.6 %tile.9 = bf16[131328]{0:T(1024)(128)(2,1)S(1)} reshape(bf16[256,513]{1,0:T(8,128)(2,1)S(1)} %tile.8) | data formatting | bytes 525312 | tf_op jit(solution)/shard_map/tile | solution.py:24
  6.3 0.0 copy-start.1
  6.3 0.2 reshape.38
  6.5 0.0 copy-done.3
  6.5 0.6 %stack.4.coef_ref = f32[5,128]{1,0:T(8,128)} concatenate(f32[1,128]{1,0:T(1,128)S(1)} %get-tuple-element.14, f32[1,128]{1,0:T(1,128)S(1)} %get-tuple-element.9, f32[1,128]{1,0:T(1,128)S(1)} %get-tuple-element.15, f32[1,128]{1,0:T(1,128)S(1)} %get-tuple-element.8, f32[1,128]{1,0:T(1,128)S(1)} %fusion.14), dimensions={0} | concatenate | bytes 5120 | tf_op jit(solution)/shard_map/stack | solution.py:168
  7.2 0.0 collective-permute-done
  7.2 0.0 copy-done.1
  7.2 0.4 %broadcast_select_fusion = bf16[2,2,32768]{2,1,0:T(2,128)(2,1)S(1)} fusion(pred[]{:T(512)S(6)} %eq.3, bf16[2,2,16384]{2,1,0:T(2,128)(2,1)S(1)} %collective-permute-done, bf16[2,2,16384]{2,1,0:T(2,128)(2,1)S(1)} %copy-done.1), kind=kLoop, calls=%fused_computation.4 | loop fusion | flops 1179648 | bytes 524289 | tf_op jit(solution)/shard_map/jit(_where)/select_n | solution.py:151
  7.6 0.2 pad.6
  7.8 0.2 reshape.36
  8.0 0.2 fusion.16
  8.2 0.1 maximum_bitcast_fusion
  8.3 0.6 %copy.14 = bf16[2,272,2,384]{3,2,1,0:T(2,128)(2,1)S(1)} copy(bf16[2,272,2,384]{3,1,2,0:T(8,128)(2,1)S(1)} %maximum_bitcast_fusion) | data formatting | bytes 1671168 | tf_op jit(solution)/shard_map/transpose | solution.py:47
  9.0 0.1 copy.19
  9.1 1.2 %convolution_reduce-precision_fusion = f32[544,256]{1,0:T(8,128)} fusion(bf16[544,768]{1,0:T(8,128)(2,1)S(1)} %bitcast.49, bf16[384,128]{0,1:T(8,128)(2,1)S(1)} %slice.70, bf16[384,128]{0,1:T(8,128)(2,1)S(1)} %slice.71, bf16[384,128]{0,1:T(8,128)(2,1)S(1)} %negate_convert_fusion), kind=kOutput, calls=%fused_computation | convolution fusion | flops 215621632 | bytes 1687552 | tf_op jit(solution)/shard_map/dot_general | solution.py:48
  10.3 4.4 %shard_map.100 = bf16[224,8,128]{2,1,0:T(8,128)(2,1)} custom-call(s32[128]{0:T(128)} %bitcast.54, s32[128]{0:T(128)} %bitcast.55, s32[128]{0:T(128)} %bitcast.56, f32[5,128]{1,0:T(8,128)} %stack.4.coef_ref, f32[2,272,256]{2,1,0:T(8,128)} %bitcast.50), custom_call_target="tpu_custom_call" | custom-call | tf_op jit(solution)/shard_map/pallas_call | solution.py:111
  14.7 5.6 %all-to-all-start = ((bf16[32,7,8,128]{3,2,1,0:T(8,128)(2,1)}), bf16[32,7,8,128]{3,2,1,0:T(8,128)(2,1)S(1)}, u32[]{:S(2)}, u32[]{:S(2)}) async-start(bf16[32,7,8,128]{3,2,1,0:T(8,128)(2,1)} %bitcast.46), calls=%async_computation | async-start | bytes 917504 | tf_op jit(solution)/shard_map/all_to_all | solution.py:173
  20.3 0.0 copy-done
  20.3 0.2 fusion.9
  20.5 14.3 %all-to-all-done = bf16[32,7,8,128]{3,2,1,0:T(8,128)(2,1)S(1)} async-done(((bf16[32,7,8,128]{3,2,1,0:T(8,128)(2,1)}), bf16[32,7,8,128]{3,2,1,0:T(8,128)(2,1)S(1)}, u32[]{:S(2)}, u32[]{:S(2)}) %all-to-all-start) | async-done | bytes 458784 | tf_op jit(solution)/shard_map/all_to_all | solution.py:173
  34.9 0.2 dot_general.16
  35.1 0.1 reshape.42
  35.2 0.2 fusion
  35.4 0.9 %copy.17 = f32[64,2,512]{2,1,0:T(2,128)} copy(f32[64,2,512]{2,0,1:T(8,128)S(1)} %fusion) | data formatting | bytes 524288 | tf_op jit(solution)/shard_map/add | solution.py:187
  (17 shorter events, 0.2 us)
Async XLA Ops:
  0.0 20.3 %copy-start = (bf16[32,2,512]{2,1,0:T(2,128)(2,1)S(1)}, bf16[32,2,512]{2,1,0:T(2,128)(2,1)}, u32[]{:S(2)}) copy-start(bf16[32,2,512]{2,1,0:T(2,128)(2,1)} %param.18) | copy-start | bytes 196612
  0.0 7.2 %collective-permute-start = (bf16[2,2,16384]{2,1,0:T(2,128)(2,1)}, bf16[2,2,16384]{2,1,0:T(2,128)(2,1)S(1)}, u32[]{:S(2)}, u32[]{:S(2)}) collective-permute-start(bf16[2,2,16384]{2,1,0:T(2,128)(2,1)} %param.10), channel_id=1, source_target_pairs={{0,1},{1,0},{2,3},{3,2},{4,5},{5,4},{6,7},{7,6},{8,9},{9,8},{10,11... | collective-permute-start | bytes 393224 | tf_op jit(solution)/shard_map/ppermute | solution.py:149
  5.7 0.9 %copy-start.3 = (f32[1,128]{1,0:T(1,128)S(1)}, f32[1,128]{1,0:T(1,128)}, u32[]{:S(2)}) copy-start(f32[1,128]{1,0:T(1,128)} %param.16) | copy-start | bytes 1540
  6.3 0.9 %copy-start.1 = (bf16[2,2,16384]{2,1,0:T(2,128)(2,1)S(1)}, bf16[2,2,16384]{2,1,0:T(2,128)(2,1)}, u32[]{:S(2)}) copy-start(bf16[2,2,16384]{2,1,0:T(2,128)(2,1)} %param.10) | copy-start | bytes 393220
  10.3 10.0 %copy-start.2 = (bf16[64,32]{0,1:T(8,128)(2,1)S(1)}, bf16[64,32]{0,1:T(8,128)(2,1)}, u32[]{:S(2)}) copy-start(bf16[64,32]{0,1:T(8,128)(2,1)} %param.19) | copy-start | bytes 12292
  14.7 20.1 %all-to-all-start = ((bf16[32,7,8,128]{3,2,1,0:T(8,128)(2,1)}), bf16[32,7,8,128]{3,2,1,0:T(8,128)(2,1)S(1)}, u32[]{:S(2)}, u32[]{:S(2)}) async-start(bf16[32,7,8,128]{3,2,1,0:T(8,128)(2,1)} %bitcast.46), calls=%async_computation | async-start | bytes 917504 | tf_op jit(solution)/shard_map/all_to_all | solution.py:173

commit v7 on v6

--- a/solution.py
+++ b/solution.py
@@ -101,7 +101,7 @@
         out_ref[base_slot + rank] = tile.astype(out_ref.dtype)
         return carry
 
-    lax.fori_loop(0, slots, record, 0, unroll=8)
+    lax.fori_loop(0, slots, record, 0, unroll=16)
 
 
 def form_payload(prof, starts, owners, dest_rows, coef, owner_total, capacity, out_rows):

time: 36.6 us -> 36.3 us (level)
  transfers between devices with their start and end apart: 2 -> 2, of which waited for: 1 -> 1; matrix products, arithmetic and copies ran while one was open for 12% -> 13% of each run, Pallas kernels for 0% -> 0%
where the time goes in v7:
time: 36.3 us; the launch traced here: 36 us
  waiting for transfers between devices  14.3 us (39%)
  starting transfers between devices  7.64 us (21%)
  local copies, waits for them, and re-layouts  4.68 us (13%)
  Pallas kernels  4.06 us (11%)
  other arithmetic  2.71 us (7%)
  matrix products  1.65 us (5%)
  between operations  0.94 us (3%)
    all_to_all x1, waiting for transfers between devices, on_device(): lax.all_to_all(outgoing.reshape(owner_total, per_owner, GROUP, LANE), axe...  14.3 us
    all_to_all x1, starting transfers between devices, on_device(): lax.all_to_all(outgoing.reshape(owner_total, per_owner, GROUP, LANE), axe...  5.59 us
    pallas_call x1, Pallas kernels, form_payload(): pl.pallas_call(kernel, out_shape=jax.ShapeDtypeStruct((owner_total * (cap...  4.06 us
    ppermute x1, starting transfers between devices, on_device(): other = lax.ppermute(echo, 'range', [(0, 1), (1, 0)])  2.06 us
    dot_general x1, matrix products, compress_chunks(): jnp.dot(windows, filter_matrix, preferred_element_type=jnp.float32)  1.22 us
    another operation x4, local copies, waits for them, and re-layouts, banded(): jnp.tile(padded, tap_count)[:2 * tap_count * tap_count]  1.18 us
    add x1, local copies, waits for them, and re-layouts, on_device(): return fine + gathered  0.91 us
  transfers between devices with their start and end apart: 2, of which 1 were waited for; matrix products, arithmetic and copies ran while one was open for 13% of the time, Pallas kernels for 0%

profile of v7, /device:TPU:1, one launch (start us, length us, event | category | flops | bytes accessed | tf_op | source)
XLA Modules:
  0.0 36.0 jit_solution(17930316494557336594)
XLA Ops:
  0.0 0.0 copy-start
  0.0 2.1 %collective-permute-start = (bf16[2,2,16384]{2,1,0:T(2,128)(2,1)}, bf16[2,2,16384]{2,1,0:T(2,128)(2,1)S(1)}, u32[]{:S(2)}, u32[]{:S(2)}) collective-permute-start(bf16[2,2,16384]{2,1,0:T(2,128)(2,1)} %param.10), channel_id=1, source_target_pairs={{0,1},{1,0},{2,3},{3,2},{4,5},{5,4},{6,7},{7,6},{8,9},{9,8},{10,11... | collective-permute-start | bytes 393224 | tf_op jit(solution)/shard_map/ppermute | solution.py:149
  2.1 0.7 %sine_multiply_fusion = f32[256]{0:T(256)S(1)} fusion(f32[256]{0:T(256)} %param.11), kind=kLoop, calls=%fused_computation.24 | loop fusion | flops 256 | bytes 2048 | tf_op jit(solution)/shard_map/mul | solution.py:19
  2.8 0.7 %cosine_multiply_fusion = bf16[256]{0:T(256)(128)(2,1)S(1)} fusion(f32[256]{0:T(256)} %param.11), kind=kLoop, calls=%fused_computation.25 | loop fusion | flops 512 | bytes 1536 | tf_op jit(solution)/shard_map/mul | solution.py:18
  3.5 0.7 %reduce-precision_bitcast_fusion = (f32[2,128]{1,0:T(2,128)S(1)}, f32[2,128]{1,0:T(2,128)S(1)}) fusion(f32[1,128,2]{1,2,0:T(2,128)} %param.12), kind=kLoop, calls=%fused_computation.26 | loop fusion | flops 512 | bytes 3072 | tf_op jit(solution)/shard_map/reduce_precision | solution.py:167
  4.9 0.5 %tile.21 = f32[131328]{0:T(1024)S(1)} reshape(f32[256,513]{1,0:T(8,128)S(1)} %tile.20) | data formatting | bytes 1050624 | tf_op jit(solution)/shard_map/tile | solution.py:24
  5.5 0.1 reshape.39
  5.7 0.0 copy-start.3
  5.7 0.6 %tile.9 = bf16[131328]{0:T(1024)(128)(2,1)S(1)} reshape(bf16[256,513]{1,0:T(8,128)(2,1)S(1)} %tile.8) | data formatting | bytes 525312 | tf_op jit(solution)/shard_map/tile | solution.py:24
  6.3 0.0 copy-start.1
  6.3 0.2 reshape.38
  6.5 0.0 copy-done.3
  6.5 0.6 %stack.4.coef_ref = f32[5,128]{1,0:T(8,128)} concatenate(f32[1,128]{1,0:T(1,128)S(1)} %get-tuple-element.14, f32[1,128]{1,0:T(1,128)S(1)} %get-tuple-element.9, f32[1,128]{1,0:T(1,128)S(1)} %get-tuple-element.15, f32[1,128]{1,0:T(1,128)S(1)} %get-tuple-element.8, f32[1,128]{1,0:T(1,128)S(1)} %fusion.14), dimensions={0} | concatenate | bytes 5120 | tf_op jit(solution)/shard_map/stack | solution.py:168
  7.2 0.0 collective-permute-done
  7.2 0.0 copy-done.1
  7.2 0.4 %broadcast_select_fusion = bf16[2,2,32768]{2,1,0:T(2,128)(2,1)S(1)} fusion(pred[]{:T(512)S(6)} %eq.3, bf16[2,2,16384]{2,1,0:T(2,128)(2,1)S(1)} %collective-permute-done, bf16[2,2,16384]{2,1,0:T(2,128)(2,1)S(1)} %copy-done.1), kind=kLoop, calls=%fused_computation.4 | loop fusion | flops 1179648 | bytes 524289 | tf_op jit(solution)/shard_map/jit(_where)/select_n | solution.py:151
  7.6 0.2 pad.6
  7.8 0.2 reshape.36
  8.0 0.2 fusion.16
  8.2 0.1 maximum_bitcast_fusion
  8.3 0.6 %copy.14 = bf16[2,272,2,384]{3,2,1,0:T(2,128)(2,1)S(1)} copy(bf16[2,272,2,384]{3,1,2,0:T(8,128)(2,1)S(1)} %maximum_bitcast_fusion) | data formatting | bytes 1671168 | tf_op jit(solution)/shard_map/transpose | solution.py:47
  9.0 0.1 copy.19
  9.1 1.2 %convolution_reduce-precision_fusion = f32[544,256]{1,0:T(8,128)} fusion(bf16[544,768]{1,0:T(8,128)(2,1)S(1)} %bitcast.49, bf16[384,128]{0,1:T(8,128)(2,1)S(1)} %slice.70, bf16[384,128]{0,1:T(8,128)(2,1)S(1)} %slice.71, bf16[384,128]{0,1:T(8,128)(2,1)S(1)} %negate_convert_fusion), kind=kOutput, calls=%fused_computation | convolution fusion | flops 215621632 | bytes 1687552 | tf_op jit(solution)/shard_map/dot_general | solution.py:48
  10.3 4.1 %shard_map.100 = bf16[224,8,128]{2,1,0:T(8,128)(2,1)} custom-call(s32[128]{0:T(128)} %bitcast.54, s32[128]{0:T(128)} %bitcast.55, s32[128]{0:T(128)} %bitcast.56, f32[5,128]{1,0:T(8,128)} %stack.4.coef_ref, f32[2,272,256]{2,1,0:T(8,128)} %bitcast.50), custom_call_target="tpu_custom_call" | custom-call | tf_op jit(solution)/shard_map/pallas_call | solution.py:111
  14.4 5.6 %all-to-all-start = ((bf16[32,7,8,128]{3,2,1,0:T(8,128)(2,1)}), bf16[32,7,8,128]{3,2,1,0:T(8,128)(2,1)S(1)}, u32[]{:S(2)}, u32[]{:S(2)}) async-start(bf16[32,7,8,128]{3,2,1,0:T(8,128)(2,1)} %bitcast.46), calls=%async_computation | async-start | bytes 917504 | tf_op jit(solution)/shard_map/all_to_all | solution.py:173
  20.0 0.0 copy-done
  20.0 0.2 fusion.9
  20.2 14.3 %all-to-all-done = bf16[32,7,8,128]{3,2,1,0:T(8,128)(2,1)S(1)} async-done(((bf16[32,7,8,128]{3,2,1,0:T(8,128)(2,1)}), bf16[32,7,8,128]{3,2,1,0:T(8,128)(2,1)S(1)}, u32[]{:S(2)}, u32[]{:S(2)}) %all-to-all-start) | async-done | bytes 458784 | tf_op jit(solution)/shard_map/all_to_all | solution.py:173
  34.5 0.2 dot_general.16
  34.7 0.1 reshape.42
  34.8 0.2 fusion
  35.1 0.9 %copy.17 = f32[64,2,512]{2,1,0:T(2,128)} copy(f32[64,2,512]{2,0,1:T(8,128)S(1)} %fusion) | data formatting | bytes 524288 | tf_op jit(solution)/shard_map/add | solution.py:187
  (17 shorter events, 0.2 us)
Async XLA Ops:
  0.0 20.0 %copy-start = (bf16[32,2,512]{2,1,0:T(2,128)(2,1)S(1)}, bf16[32,2,512]{2,1,0:T(2,128)(2,1)}, u32[]{:S(2)}) copy-start(bf16[32,2,512]{2,1,0:T(2,128)(2,1)} %param.18) | copy-start | bytes 196612
  0.0 7.2 %collective-permute-start = (bf16[2,2,16384]{2,1,0:T(2,128)(2,1)}, bf16[2,2,16384]{2,1,0:T(2,128)(2,1)S(1)}, u32[]{:S(2)}, u32[]{:S(2)}) collective-permute-start(bf16[2,2,16384]{2,1,0:T(2,128)(2,1)} %param.10), channel_id=1, source_target_pairs={{0,1},{1,0},{2,3},{3,2},{4,5},{5,4},{6,7},{7,6},{8,9},{9,8},{10,11... | collective-permute-start | bytes 393224 | tf_op jit(solution)/shard_map/ppermute | solution.py:149
  5.7 0.9 %copy-start.3 = (f32[1,128]{1,0:T(1,128)S(1)}, f32[1,128]{1,0:T(1,128)}, u32[]{:S(2)}) copy-start(f32[1,128]{1,0:T(1,128)} %param.16) | copy-start | bytes 1540
  6.3 0.9 %copy-start.1 = (bf16[2,2,16384]{2,1,0:T(2,128)(2,1)S(1)}, bf16[2,2,16384]{2,1,0:T(2,128)(2,1)}, u32[]{:S(2)}) copy-start(bf16[2,2,16384]{2,1,0:T(2,128)(2,1)} %param.10) | copy-start | bytes 393220
  10.3 9.7 %copy-start.2 = (bf16[64,32]{0,1:T(8,128)(2,1)S(1)}, bf16[64,32]{0,1:T(8,128)(2,1)}, u32[]{:S(2)}) copy-start(bf16[64,32]{0,1:T(8,128)(2,1)} %param.19) | copy-start | bytes 12292
  14.4 20.1 %all-to-all-start = ((bf16[32,7,8,128]{3,2,1,0:T(8,128)(2,1)}), bf16[32,7,8,128]{3,2,1,0:T(8,128)(2,1)S(1)}, u32[]{:S(2)}, u32[]{:S(2)}) async-start(bf16[32,7,8,128]{3,2,1,0:T(8,128)(2,1)} %bitcast.46), calls=%async_computation | async-start | bytes 917504 | tf_op jit(solution)/shard_map/all_to_all | solution.py:173

commit v8 on v7

--- a/solution.py
+++ b/solution.py
@@ -148,8 +148,8 @@
     if range_count == 2:
         other = lax.ppermute(echo, "range", [(0, 1), (1, 0)])
         first = lax.axis_index("range") == 0
-        raw_echo = jnp.where(
-            first, jnp.concatenate([echo, other], axis=2), jnp.concatenate([other, echo], axis=2)
+        raw_echo = jnp.concatenate(
+            [jnp.where(first, echo, other), jnp.where(first, other, echo)], axis=2
         )
     else:
         raw_echo = lax.all_gather(echo, "range", axis=2, tiled=True)

time: 36.3 us -> 36.1 us (level)
  no operation moved by 1% of the time
where the time goes in v8:
time: 36.1 us; the launch traced here: 35.8 us
  waiting for transfers between devices  14.3 us (40%)
  starting transfers between devices  7.64 us (21%)
  local copies, waits for them, and re-layouts  4.48 us (12%)
  Pallas kernels  4.06 us (11%)
  other arithmetic  2.75 us (8%)
  matrix products  1.66 us (5%)
  between operations  0.94 us (3%)
    all_to_all x1, waiting for transfers between devices, on_device(): lax.all_to_all(outgoing.reshape(owner_total, per_owner, GROUP, LANE), axe...  14.3 us
    all_to_all x1, starting transfers between devices, on_device(): lax.all_to_all(outgoing.reshape(owner_total, per_owner, GROUP, LANE), axe...  5.59 us
    pallas_call x1, Pallas kernels, form_payload(): pl.pallas_call(kernel, out_shape=jax.ShapeDtypeStruct((owner_total * (cap...  4.06 us
    ppermute x1, starting transfers between devices, on_device(): other = lax.ppermute(echo, 'range', [(0, 1), (1, 0)])  2.06 us
    dot_general x1, matrix products, compress_chunks(): jnp.dot(windows, filter_matrix, preferred_element_type=jnp.float32)  1.23 us
    another operation x4, local copies, waits for them, and re-layouts, banded(): jnp.tile(padded, tap_count)[:2 * tap_count * tap_count]  1.18 us
    add x1, local copies, waits for them, and re-layouts, on_device(): return fine + gathered  0.91 us
    mul x1, other arithmetic, chirp_matrix(): real_taps = jnp.cos(chirp_phase) * tap_scale  0.72 us
  transfers between devices with their start and end apart: 2, of which 1 were waited for; matrix products, arithmetic and copies ran while one was open for 13% of the time, Pallas kernels for 0%

profile of v8, /device:TPU:1, one launch (start us, length us, event | category | flops | bytes accessed | tf_op | source)
XLA Modules:
  0.0 35.8 jit_solution(1095567787749806774)
XLA Ops:
  0.0 0.0 copy-start
  0.0 2.1 %collective-permute-start = (bf16[2,2,16384]{2,1,0:T(2,128)(2,1)}, bf16[2,2,16384]{2,1,0:T(2,128)(2,1)S(1)}, u32[]{:S(2)}, u32[]{:S(2)}) collective-permute-start(bf16[2,2,16384]{2,1,0:T(2,128)(2,1)} %param.10), channel_id=1, source_target_pairs={{0,1},{1,0},{2,3},{3,2},{4,5},{5,4},{6,7},{7,6},{8,9},{9,8},{10,11... | collective-permute-start | bytes 393224 | tf_op jit(solution)/shard_map/ppermute | solution.py:149
  2.1 0.7 %sine_multiply_fusion = f32[256]{0:T(256)S(1)} fusion(f32[256]{0:T(256)} %param.11), kind=kLoop, calls=%fused_computation.29 | loop fusion | flops 256 | bytes 2048 | tf_op jit(solution)/shard_map/mul | solution.py:19
  2.8 0.7 %cosine_multiply_fusion = bf16[256]{0:T(256)(128)(2,1)S(1)} fusion(f32[256]{0:T(256)} %param.11), kind=kLoop, calls=%fused_computation.30 | loop fusion | flops 512 | bytes 1536 | tf_op jit(solution)/shard_map/mul | solution.py:18
  3.5 0.7 %reduce-precision_bitcast_fusion = (f32[2,128]{1,0:T(2,128)S(1)}, f32[2,128]{1,0:T(2,128)S(1)}) fusion(f32[1,128,2]{1,2,0:T(2,128)} %param.12), kind=kLoop, calls=%fused_computation.31 | loop fusion | flops 512 | bytes 3072 | tf_op jit(solution)/shard_map/reduce_precision | solution.py:167
  4.9 0.5 %tile.21 = f32[131328]{0:T(1024)S(1)} reshape(f32[256,513]{1,0:T(8,128)S(1)} %tile.20) | data formatting | bytes 1050624 | tf_op jit(solution)/shard_map/tile | solution.py:24
  5.5 0.1 reshape.39
  5.7 0.0 copy-start.3
  5.7 0.6 %tile.9 = bf16[131328]{0:T(1024)(128)(2,1)S(1)} reshape(bf16[256,513]{1,0:T(8,128)(2,1)S(1)} %tile.8) | data formatting | bytes 525312 | tf_op jit(solution)/shard_map/tile | solution.py:24
  6.3 0.0 copy-start.1
  6.3 0.2 reshape.38
  6.5 0.0 copy-done.3
  6.5 0.6 %stack.4.coef_ref = f32[5,128]{1,0:T(8,128)} concatenate(f32[1,128]{1,0:T(1,128)S(1)} %get-tuple-element.16, f32[1,128]{1,0:T(1,128)S(1)} %get-tuple-element.11, f32[1,128]{1,0:T(1,128)S(1)} %get-tuple-element.17, f32[1,128]{1,0:T(1,128)S(1)} %get-tuple-element.10, f32[1,128]{1,0:T(1,128)S(1)} %fusion.17), dimensions={0} | concatenate | bytes 5120 | tf_op jit(solution)/shard_map/stack | solution.py:168
  7.2 0.0 collective-permute-done
  7.2 0.0 copy-done.1
  7.2 0.2 broadcast_select_fusion.1
  7.4 0.2 fusion.11
  7.7 0.2 reshape.36
  7.9 0.2 fusion.19
  8.0 0.1 maximum_bitcast_fusion
  8.1 0.6 %copy.14 = bf16[2,272,2,384]{3,2,1,0:T(2,128)(2,1)S(1)} copy(bf16[2,272,2,384]{3,1,2,0:T(8,128)(2,1)S(1)} %maximum_bitcast_fusion) | data formatting | bytes 1671168 | tf_op jit(solution)/shard_map/transpose | solution.py:47
  8.8 0.1 copy.19
  8.9 1.2 %convolution_reduce-precision_fusion = f32[544,256]{1,0:T(8,128)} fusion(bf16[544,768]{1,0:T(8,128)(2,1)S(1)} %bitcast.49, bf16[384,128]{0,1:T(8,128)(2,1)S(1)} %slice.70, bf16[384,128]{0,1:T(8,128)(2,1)S(1)} %slice.71, bf16[384,128]{0,1:T(8,128)(2,1)S(1)} %negate_convert_fusion), kind=kOutput, calls=%fused_computation | convolution fusion | flops 215621632 | bytes 1687552 | tf_op jit(solution)/shard_map/dot_general | solution.py:48
  10.2 4.1 %shard_map.100 = bf16[224,8,128]{2,1,0:T(8,128)(2,1)} custom-call(s32[128]{0:T(128)} %bitcast.54, s32[128]{0:T(128)} %bitcast.55, s32[128]{0:T(128)} %bitcast.56, f32[5,128]{1,0:T(8,128)} %stack.4.coef_ref, f32[2,272,256]{2,1,0:T(8,128)} %bitcast.50), custom_call_target="tpu_custom_call" | custom-call | tf_op jit(solution)/shard_map/pallas_call | solution.py:111
  14.2 5.6 %all-to-all-start = ((bf16[32,7,8,128]{3,2,1,0:T(8,128)(2,1)}), bf16[32,7,8,128]{3,2,1,0:T(8,128)(2,1)S(1)}, u32[]{:S(2)}, u32[]{:S(2)}) async-start(bf16[32,7,8,128]{3,2,1,0:T(8,128)(2,1)} %bitcast.46), calls=%async_computation | async-start | bytes 917504 | tf_op jit(solution)/shard_map/all_to_all | solution.py:173
  19.8 0.0 copy-done
  19.8 0.2 fusion.12
  20.0 14.3 %all-to-all-done = bf16[32,7,8,128]{3,2,1,0:T(8,128)(2,1)S(1)} async-done(((bf16[32,7,8,128]{3,2,1,0:T(8,128)(2,1)}), bf16[32,7,8,128]{3,2,1,0:T(8,128)(2,1)S(1)}, u32[]{:S(2)}, u32[]{:S(2)}) %all-to-all-start) | async-done | bytes 458784 | tf_op jit(solution)/shard_map/all_to_all | solution.py:173
  34.4 0.2 dot_general.16
  34.6 0.1 reshape.42
  34.7 0.2 fusion
  34.9 0.9 %copy.17 = f32[64,2,512]{2,1,0:T(2,128)} copy(f32[64,2,512]{2,0,1:T(8,128)S(1)} %fusion) | data formatting | bytes 524288 | tf_op jit(solution)/shard_map/add | solution.py:187
  (17 shorter events, 0.2 us)
Async XLA Ops:
  0.0 19.8 %copy-start = (bf16[32,2,512]{2,1,0:T(2,128)(2,1)S(1)}, bf16[32,2,512]{2,1,0:T(2,128)(2,1)}, u32[]{:S(2)}) copy-start(bf16[32,2,512]{2,1,0:T(2,128)(2,1)} %param.18) | copy-start | bytes 196612
  0.0 7.2 %collective-permute-start = (bf16[2,2,16384]{2,1,0:T(2,128)(2,1)}, bf16[2,2,16384]{2,1,0:T(2,128)(2,1)S(1)}, u32[]{:S(2)}, u32[]{:S(2)}) collective-permute-start(bf16[2,2,16384]{2,1,0:T(2,128)(2,1)} %param.10), channel_id=1, source_target_pairs={{0,1},{1,0},{2,3},{3,2},{4,5},{5,4},{6,7},{7,6},{8,9},{9,8},{10,11... | collective-permute-start | bytes 393224 | tf_op jit(solution)/shard_map/ppermute | solution.py:149
  5.7 0.9 %copy-start.3 = (f32[1,128]{1,0:T(1,128)S(1)}, f32[1,128]{1,0:T(1,128)}, u32[]{:S(2)}) copy-start(f32[1,128]{1,0:T(1,128)} %param.16) | copy-start | bytes 1540
  6.3 0.9 %copy-start.1 = (bf16[2,2,16384]{2,1,0:T(2,128)(2,1)S(1)}, bf16[2,2,16384]{2,1,0:T(2,128)(2,1)}, u32[]{:S(2)}) copy-start(bf16[2,2,16384]{2,1,0:T(2,128)(2,1)} %param.10) | copy-start | bytes 393220
  10.2 9.7 %copy-start.2 = (bf16[64,32]{0,1:T(8,128)(2,1)S(1)}, bf16[64,32]{0,1:T(8,128)(2,1)}, u32[]{:S(2)}) copy-start(bf16[64,32]{0,1:T(8,128)(2,1)} %param.19) | copy-start | bytes 12292
  14.2 20.1 %all-to-all-start = ((bf16[32,7,8,128]{3,2,1,0:T(8,128)(2,1)}), bf16[32,7,8,128]{3,2,1,0:T(8,128)(2,1)S(1)}, u32[]{:S(2)}, u32[]{:S(2)}) async-start(bf16[32,7,8,128]{3,2,1,0:T(8,128)(2,1)} %bitcast.46), calls=%async_computation | async-start | bytes 917504 | tf_op jit(solution)/shard_map/all_to_all | solution.py:173

commit v9 on v8

--- a/solution.py
+++ b/solution.py
@@ -86,9 +86,9 @@
             rows = pltpu.roll(rows, lift, 0)[:GROUP]
             parts.append((rows[:, :LANE], rows[:, LANE:]))
         (re0, im0), (re1, im1) = parts
-        c0, s0, c1, s1, sc = (coef_ref[i, j] for i in range(5))
-        out_re = ((c0 * re0 + c1 * re1) - (s0 * im0 + s1 * im1)) * sc
-        out_im = ((c0 * im0 + c1 * im1) + (s0 * re0 + s1 * re1)) * sc
+        c0, s0, c1, s1 = (coef_ref[i, j] for i in range(4))
+        out_re = (c0 * re0 + c1 * re1) - (s0 * im0 + s1 * im1)
+        out_im = (c0 * im0 + c1 * im1) + (s0 * re0 + s1 * re1)
         turn = (LANE - off) & (LANE - 1)
         keep = lane_ids < LANE - off
         shifted = []
@@ -165,7 +165,7 @@
     turns = phases.T
     cosine = lax.reduce_precision(jnp.cos(turns), 8, 7)
     sine_part = lax.reduce_precision(jnp.sin(turns), 8, 7)
-    coef = jnp.stack([cosine[0], sine_part[0], cosine[1], sine_part[1], scales])
+    coef = jnp.stack([cosine[0], sine_part[0], cosine[1], sine_part[1]]) * scales[None, :]
 
     outgoing = form_payload(
         prof, starts, owners, dest_rows, coef, owner_total, capacity, out_rows

time: 36.1 us -> 35.7 us (0.989)
  other arithmetic: 2.75 us -> 1.97 us
  starting transfers between devices: 7.64 us -> 8.24 us
    mul x1, other arithmetic: 0.72 us -> 0.04 us  [chirp_matrix(): real_taps = jnp.cos(chirp_phase) * tap_scale]
    reduce_precision x1, other arithmetic: 0.72 us -> 0.04 us  [on_device(): cosine = lax.reduce_precision(jnp.cos(turns), 8, 7)]
    another operation x1 -> x0, local copies, waits for them, and re-layouts: 0.61 us -> none  [on_device(): coef = jnp.stack([cosine[0], sine_part[0], cosine[1], sine_part[1], scales])]
    mul x0 -> x2, other arithmetic: none -> 0.6 us  [on_device(): jnp.stack([cosine[0], sine_part[0], cosine[1], sine_part[1]])]
    all_to_all x1, starting transfers between devices: 5.59 us -> 6.18 us  [on_device(): lax.all_to_all(outgoing.reshape(owner_total, per_owner, GROUP, LANE), axe...]
    unnamed x10 -> x14, local copies, waits for them, and re-layouts: 0.17 us -> 0.7 us
  transfers between devices with their start and end apart: 2 -> 2, of which waited for: 1 -> 1; matrix products, arithmetic and copies ran while one was open for 13% -> 9% of each run, Pallas kernels for 0% -> 0%
where the time goes in v9:
time: 35.7 us; the launch traced here: 35.5 us
  waiting for transfers between devices  14.3 us (40%)
  starting transfers between devices  8.24 us (23%)
  local copies, waits for them, and re-layouts  4.41 us (12%)
  Pallas kernels  3.98 us (11%)
  other arithmetic  1.97 us (6%)
  matrix products  1.65 us (5%)
  between operations  0.94 us (3%)
    all_to_all x1, waiting for transfers between devices, on_device(): lax.all_to_all(outgoing.reshape(owner_total, per_owner, GROUP, LANE), axe...  14.3 us
    all_to_all x1, starting transfers between devices, on_device(): lax.all_to_all(outgoing.reshape(owner_total, per_owner, GROUP, LANE), axe...  6.18 us
    pallas_call x1, Pallas kernels, form_payload(): pl.pallas_call(kernel, out_shape=jax.ShapeDtypeStruct((owner_total * (cap...  3.98 us
    ppermute x1, starting transfers between devices, on_device(): other = lax.ppermute(echo, 'range', [(0, 1), (1, 0)])  2.06 us
    dot_general x1, matrix products, compress_chunks(): jnp.dot(windows, filter_matrix, preferred_element_type=jnp.float32)  1.22 us
    another operation x4, local copies, waits for them, and re-layouts, banded(): jnp.tile(padded, tap_count)[:2 * tap_count * tap_count]  1.18 us
    add x1, local copies, waits for them, and re-layouts, on_device(): return fine + gathered  0.91 us
    mul x1, other arithmetic, chirp_matrix(): imag_taps = jnp.sin(chirp_phase) * tap_scale  0.72 us
  transfers between devices with their start and end apart: 2, of which 1 were waited for; matrix products, arithmetic and copies ran while one was open for 9% of the time, Pallas kernels for 0%

profile of v9, /device:TPU:1, one launch (start us, length us, event | category | flops | bytes accessed | tf_op | source)
XLA Modules:
  0.0 35.5 jit_solution(18429198130829245958)
XLA Ops:
  0.0 2.1 %collective-permute-start = (bf16[2,2,16384]{2,1,0:T(2,128)(2,1)}, bf16[2,2,16384]{2,1,0:T(2,128)(2,1)S(1)}, u32[]{:S(2)}, u32[]{:S(2)}) collective-permute-start(bf16[2,2,16384]{2,1,0:T(2,128)(2,1)} %param.10), channel_id=1, source_target_pairs={{0,1},{1,0},{2,3},{3,2},{4,5},{5,4},{6,7},{7,6},{8,9},{9,8},{10,11... | collective-permute-start | bytes 393224 | tf_op jit(solution)/shard_map/ppermute | solution.py:149
  2.1 0.7 %sine_multiply_fusion = f32[256]{0:T(256)S(1)} fusion(f32[256]{0:T(256)} %param.11), kind=kLoop, calls=%fused_computation.30 | loop fusion | flops 256 | bytes 2048 | tf_op jit(solution)/shard_map/mul | solution.py:19
  2.8 0.5 %tile.21 = f32[131328]{0:T(1024)S(1)} reshape(f32[256,513]{1,0:T(8,128)S(1)} %tile.20) | data formatting | bytes 1050624 | tf_op jit(solution)/shard_map/tile | solution.py:24
  3.4 0.0 copy-start.4
  3.4 0.0 copy-start.3
  3.4 0.1 reshape.39
  3.6 0.5 %copy-done.4 = f32[256]{0:T(256)S(1)} copy-done((f32[256]{0:T(256)S(1)}, f32[256]{0:T(256)}, u32[]{:S(2)}) %copy-start.4) | copy-done | bytes 1048
  4.9 0.0 copy-start.5
  4.9 0.0 copy-start.1
  4.9 0.6 %tile.9 = bf16[131328]{0:T(1024)(128)(2,1)S(1)} reshape(bf16[256,513]{1,0:T(8,128)(2,1)S(1)} %tile.8) | data formatting | bytes 525312 | tf_op jit(solution)/shard_map/tile | solution.py:24
  5.5 0.2 reshape.38
  5.8 0.6 %maximum_multiply_fusion.coef_ref = f32[4,128]{1,0:T(4,128)} fusion(f32[1,128]{1,0:T(1,128)S(1)} %get-tuple-element.16, f32[1,128]{1,0:T(1,128)S(1)} %get-tuple-element.11, f32[1,128]{1,0:T(1,128)S(1)} %get-tuple-element.17, f32[1,128]{1,0:T(1,128)S(1)} %get-tuple-element.10, f32[128]{0:T(128)S(1)} %fusion.18), kind=kLoop, calls=%fused_computation.28 | loop fusion | flops 2048 | bytes 4608 | tf_op jit(solution)/shard_map/mul | solution.py:168
  6.4 0.0 collective-permute-done
  6.4 0.0 copy-done.1
  6.4 0.2 broadcast_select_fusion.1
  6.6 0.2 fusion.11
  6.8 0.2 reshape.36
  7.0 0.2 fusion.20
  7.2 0.1 maximum_bitcast_fusion
  7.3 0.6 %copy.14 = bf16[2,272,2,384]{3,2,1,0:T(2,128)(2,1)S(1)} copy(bf16[2,272,2,384]{3,1,2,0:T(8,128)(2,1)S(1)} %maximum_bitcast_fusion) | data formatting | bytes 1671168 | tf_op jit(solution)/shard_map/transpose | solution.py:47
  7.9 0.1 copy.19
  8.1 1.2 %convolution_reduce-precision_fusion = f32[544,256]{1,0:T(8,128)} fusion(bf16[544,768]{1,0:T(8,128)(2,1)S(1)} %bitcast.51, bf16[384,128]{0,1:T(8,128)(2,1)S(1)} %slice.70, bf16[384,128]{0,1:T(8,128)(2,1)S(1)} %slice.71, bf16[384,128]{0,1:T(8,128)(2,1)S(1)} %negate_convert_fusion), kind=kOutput, calls=%fused_computation | convolution fusion | flops 215621632 | bytes 1687552 | tf_op jit(solution)/shard_map/dot_general | solution.py:48
  9.3 4.0 %shard_map.100 = bf16[224,8,128]{2,1,0:T(8,128)(2,1)} custom-call(s32[128]{0:T(128)} %bitcast.56, s32[128]{0:T(128)} %bitcast.57, s32[128]{0:T(128)} %bitcast.58, f32[4,128]{1,0:T(4,128)} %maximum_multiply_fusion.coef_ref, f32[2,272,256]{2,1,0:T(8,128)} %bitcast.52), custom_call_target="tpu_custom_call" | custom-call | tf_op jit(solution)/shard_map/pallas_call | solution.py:111
  13.3 6.2 %all-to-all-start = ((bf16[32,7,8,128]{3,2,1,0:T(8,128)(2,1)}), bf16[32,7,8,128]{3,2,1,0:T(8,128)(2,1)S(1)}, u32[]{:S(2)}, u32[]{:S(2)}) async-start(bf16[32,7,8,128]{3,2,1,0:T(8,128)(2,1)} %bitcast.48), calls=%async_computation | async-start | bytes 917504 | tf_op jit(solution)/shard_map/all_to_all | solution.py:173
  19.5 0.0 copy-done
  19.5 0.0 copy-done.2
  19.5 0.2 fusion.12
  19.7 14.3 %all-to-all-done = bf16[32,7,8,128]{3,2,1,0:T(8,128)(2,1)S(1)} async-done(((bf16[32,7,8,128]{3,2,1,0:T(8,128)(2,1)}), bf16[32,7,8,128]{3,2,1,0:T(8,128)(2,1)S(1)}, u32[]{:S(2)}, u32[]{:S(2)}) %all-to-all-start) | async-done | bytes 458784 | tf_op jit(solution)/shard_map/all_to_all | solution.py:173
  34.0 0.2 dot_general.16
  34.2 0.1 reshape.42
  34.3 0.2 fusion
  34.6 0.9 %copy.17 = f32[64,2,512]{2,1,0:T(2,128)} copy(f32[64,2,512]{2,0,1:T(8,128)S(1)} %fusion) | data formatting | bytes 524288 | tf_op jit(solution)/shard_map/add | solution.py:187
  (21 shorter events, 0.3 us)
Async XLA Ops:
  0.0 19.5 %copy-start = (bf16[32,2,512]{2,1,0:T(2,128)(2,1)S(1)}, bf16[32,2,512]{2,1,0:T(2,128)(2,1)}, u32[]{:S(2)}) copy-start(bf16[32,2,512]{2,1,0:T(2,128)(2,1)} %param.18) | copy-start | bytes 196612
  0.0 6.4 %collective-permute-start = (bf16[2,2,16384]{2,1,0:T(2,128)(2,1)}, bf16[2,2,16384]{2,1,0:T(2,128)(2,1)S(1)}, u32[]{:S(2)}, u32[]{:S(2)}) collective-permute-start(bf16[2,2,16384]{2,1,0:T(2,128)(2,1)} %param.10), channel_id=1, source_target_pairs={{0,1},{1,0},{2,3},{3,2},{4,5},{5,4},{6,7},{7,6},{8,9},{9,8},{10,11... | collective-permute-start | bytes 393224 | tf_op jit(solution)/shard_map/ppermute | solution.py:149
  3.4 0.7 %copy-start.4 = (f32[256]{0:T(256)S(1)}, f32[256]{0:T(256)}, u32[]{:S(2)}) copy-start(f32[256]{0:T(256)} %param.11) | copy-start | bytes 3076
  3.4 0.7 %copy-start.3 = (f32[1,128,2]{1,2,0:T(2,128)S(1)}, f32[1,128,2]{1,2,0:T(2,128)}, u32[]{:S(2)}) copy-start(f32[1,128,2]{1,2,0:T(2,128)} %param.12) | copy-start | bytes 3076
  4.9 0.9 %copy-start.5 = (f32[1,128]{1,0:T(1,128)S(1)}, f32[1,128]{1,0:T(1,128)}, u32[]{:S(2)}) copy-start(f32[1,128]{1,0:T(1,128)} %param.16) | copy-start | bytes 1540
  4.9 1.5 %copy-start.1 = (bf16[2,2,16384]{2,1,0:T(2,128)(2,1)S(1)}, bf16[2,2,16384]{2,1,0:T(2,128)(2,1)}, u32[]{:S(2)}) copy-start(bf16[2,2,16384]{2,1,0:T(2,128)(2,1)} %param.10) | copy-start | bytes 393220
  9.3 10.2 %copy-start.2 = (bf16[64,32]{0,1:T(8,128)(2,1)S(1)}, bf16[64,32]{0,1:T(8,128)(2,1)}, u32[]{:S(2)}) copy-start(bf16[64,32]{0,1:T(8,128)(2,1)} %param.19) | copy-start | bytes 12292
  13.3 20.7 %all-to-all-start = ((bf16[32,7,8,128]{3,2,1,0:T(8,128)(2,1)}), bf16[32,7,8,128]{3,2,1,0:T(8,128)(2,1)S(1)}, u32[]{:S(2)}, u32[]{:S(2)}) async-start(bf16[32,7,8,128]{3,2,1,0:T(8,128)(2,1)} %bitcast.48), calls=%async_computation | async-start | bytes 917504 | tf_op jit(solution)/shard_map/all_to_all | solution.py:173

commit v10 on v9

--- a/solution.py
+++ b/solution.py
@@ -41,11 +41,16 @@
         echo_full, ((0, 0), (0, 0), (0, (chunk_total + reach) * LANE - bin_count))
     )
     chunks = padded.reshape(pulses, planes, chunk_total + reach, LANE)
-    windows = jnp.concatenate(
-        [chunks[:, :, lead : lead + chunk_total] for lead in range(reach + 1)], axis=3
-    )
-    windows = windows.transpose(0, 2, 1, 3).reshape(pulses * chunk_total, -1)
-    filtered = jnp.dot(windows, filter_matrix, preferred_element_type=jnp.float32)
+    bands = filter_matrix.reshape(planes, reach + 1, LANE, -1)
+    filtered = sum(
+        jnp.einsum(
+            "kpql,plo->kqo",
+            chunks[:, :, lead : lead + chunk_total],
+            bands[:, lead],
+            preferred_element_type=jnp.float32,
+        )
+        for lead in range(reach + 1)
+    )
     filtered = lax.reduce_precision(filtered, 8, 7)
     return filtered.reshape(pulses, chunk_total, planes * LANE)
 

time: 35.7 us -> 36 us (level)
  local copies, waits for them, and re-layouts: 4.41 us -> 5.08 us
  starting transfers between devices: 8.24 us -> 7.65 us
    unnamed x14 -> x13, local copies, waits for them, and re-layouts: 0.7 us -> 2 us
    transpose x1 -> x0, local copies, waits for them, and re-layouts: 0.65 us -> none  [compress_chunks(): windows = windows.transpose(0, 2, 1, 3).reshape(pulses * chunk_total, -1)]
    all_to_all x1, starting transfers between devices: 6.18 us -> 5.59 us  [on_device(): lax.all_to_all(outgoing.reshape(owner_total, per_owner, GROUP, LANE), axe...]
    dot_general x1 -> x3, matrix products: 1.22 us -> 1.51 us  [compress_chunks(): jnp.einsum('kpql,plo->kqo', chunks[:, :, lead:lead + chunk_total], bands[...]
where the time goes in v10:
time: 36 us; the launch traced here: 35.7 us
  waiting for transfers between devices  14.3 us (40%)
  starting transfers between devices  7.65 us (21%)
  local copies, waits for them, and re-layouts  5.08 us (14%)
  Pallas kernels  3.97 us (11%)
  matrix products  1.94 us (5%)
  other arithmetic  1.89 us (5%)
  between operations  0.92 us (3%)
    all_to_all x1, waiting for transfers between devices, on_device(): lax.all_to_all(outgoing.reshape(owner_total, per_owner, GROUP, LANE), axe...  14.3 us
    all_to_all x1, starting transfers between devices, on_device(): lax.all_to_all(outgoing.reshape(owner_total, per_owner, GROUP, LANE), axe...  5.59 us
    pallas_call x1, Pallas kernels, form_payload(): pl.pallas_call(kernel, out_shape=jax.ShapeDtypeStruct((owner_total * (cap...  3.97 us
    ppermute x1, starting transfers between devices, on_device(): other = lax.ppermute(echo, 'range', [(0, 1), (1, 0)])  2.06 us
    unnamed x13, local copies, waits for them, and re-layouts  2 us
    dot_general x3, matrix products, compress_chunks(): jnp.einsum('kpql,plo->kqo', chunks[:, :, lead:lead + chunk_total], bands[...  1.51 us
    another operation x4, local copies, waits for them, and re-layouts, banded(): jnp.tile(padded, tap_count)[:2 * tap_count * tap_count]  1.18 us
    add x1, local copies, waits for them, and re-layouts, on_device(): return fine + gathered  0.91 us
  transfers between devices with their start and end apart: 2, of which 1 were waited for; matrix products, arithmetic and copies ran while one was open for 9% of the time, Pallas kernels for 0%

profile of v10, /device:TPU:1, one launch (start us, length us, event | category | flops | bytes accessed | tf_op | source)
XLA Modules:
  0.0 35.7 jit_solution(4617350828795447906)
XLA Ops:
  0.0 0.0 copy-start
  0.0 2.1 %collective-permute-start = (bf16[2,2,16384]{2,1,0:T(2,128)(2,1)}, bf16[2,2,16384]{2,1,0:T(2,128)(2,1)S(1)}, u32[]{:S(2)}, u32[]{:S(2)}) collective-permute-start(bf16[2,2,16384]{2,1,0:T(2,128)(2,1)} %param.10), channel_id=1, source_target_pairs={{0,1},{1,0},{2,3},{3,2},{4,5},{5,4},{6,7},{7,6},{8,9},{9,8},{10,11... | collective-permute-start | bytes 393224 | tf_op jit(solution)/shard_map/ppermute | solution.py:154
  2.1 0.7 %sine_multiply_fusion = f32[256]{0:T(256)S(1)} fusion(f32[256]{0:T(256)} %param.11), kind=kLoop, calls=%fused_computation.34 | loop fusion | flops 256 | bytes 2048 | tf_op jit(solution)/shard_map/mul | solution.py:19
  2.8 0.5 %tile.21 = f32[131328]{0:T(1024)S(1)} reshape(f32[256,513]{1,0:T(8,128)S(1)} %tile.20) | data formatting | bytes 1050624 | tf_op jit(solution)/shard_map/tile | solution.py:24
  3.4 0.1 reshape.35
  3.5 0.0 copy-start.4
  3.5 0.6 %copy-done.4 = f32[256]{0:T(256)S(1)} copy-done((f32[256]{0:T(256)S(1)}, f32[256]{0:T(256)}, u32[]{:S(2)}) %copy-start.4) | copy-done | bytes 1048
  4.3 0.6 %tile.9 = bf16[131328]{0:T(1024)(128)(2,1)S(1)} reshape(bf16[256,513]{1,0:T(8,128)(2,1)S(1)} %tile.8) | data formatting | bytes 525312 | tf_op jit(solution)/shard_map/tile | solution.py:24
  4.9 0.2 reshape.34
  5.1 0.0 copy-start.1
  5.2 0.2 copy.21
  5.3 0.0 copy-start.3
  5.3 0.7 %copy-done.3 = f32[1,128,2]{1,2,0:T(2,128)S(1)} copy-done((f32[1,128,2]{1,2,0:T(2,128)S(1)}, f32[1,128,2]{1,2,0:T(2,128)}, u32[]{:S(2)}) %copy-start.3) | copy-done | bytes 1048
  6.7 0.0 copy-start.5
  6.7 0.6 %copy-done.5 = f32[1,128]{1,0:T(1,128)S(1)} copy-done((f32[1,128]{1,0:T(1,128)S(1)}, f32[1,128]{1,0:T(1,128)}, u32[]{:S(2)}) %copy-start.5) | copy-done | bytes 536
  7.4 0.6 %maximum_multiply_fusion.coef_ref = f32[4,128]{1,0:T(4,128)} fusion(f32[1,128]{1,0:T(1,128)S(1)} %get-tuple-element.13, f32[1,128]{1,0:T(1,128)S(1)} %get-tuple-element.8, f32[1,128]{1,0:T(1,128)S(1)} %get-tuple-element.14, f32[1,128]{1,0:T(1,128)S(1)} %get-tuple-element.7, f32[128]{0:T(128)S(1)} %fusion.17), kind=kLoop, calls=%fused_computation.32 | loop fusion | flops 2048 | bytes 4608 | tf_op jit(solution)/shard_map/mul | solution.py:173
  8.0 0.0 collective-permute-done
  8.0 0.0 copy-done.1
  8.0 0.2 broadcast_select_fusion.1
  8.2 0.2 fusion.7
  8.4 0.2 reshape.33
  8.6 0.2 convolution_bitcast_fusion.1
  8.9 0.2 convolution_bitcast_fusion
  9.1 1.0 %fusion.2.prof_ref = f32[2,272,256]{2,1,0:T(8,128)} fusion(f32[2,272,256]{2,1,0:T(8,128)S(1)} %convolution_bitcast_fusion, f32[2,272,256]{2,1,0:T(8,128)S(1)} %convolution_bitcast_fusion.1, bf16[2,2,274,128]{3,2,1,0:T(8,128)(2,1)S(1)} %reshape.33, bf16[2,3,128,256]{3,2,1,0:T(8,128)(2,1)S(1)} %bitcast.77), kind=kOutput, calls=%fused_computation.5 | convolution fusion | flops 71720960 | bytes 2080768 | tf_op jit(solution)/shard_map/kpql,plo->kqo/dot_general | solution.py:46
  10.2 4.0 %shard_map.100 = bf16[224,8,128]{2,1,0:T(8,128)(2,1)} custom-call(s32[128]{0:T(128)} %bitcast.83, s32[128]{0:T(128)} %bitcast.84, s32[128]{0:T(128)} %bitcast.85, f32[4,128]{1,0:T(4,128)} %maximum_multiply_fusion.coef_ref, f32[2,272,256]{2,1,0:T(8,128)} %fusion.2.prof_ref), custom_call_target="tpu_custom_call" | custom-call | tf_op jit(solution)/shard_map/pallas_call | solution.py:116
  14.1 5.6 %all-to-all-start = ((bf16[32,7,8,128]{3,2,1,0:T(8,128)(2,1)}), bf16[32,7,8,128]{3,2,1,0:T(8,128)(2,1)S(1)}, u32[]{:S(2)}, u32[]{:S(2)}) async-start(bf16[32,7,8,128]{3,2,1,0:T(8,128)(2,1)} %bitcast.74), calls=%async_computation | async-start | bytes 917504 | tf_op jit(solution)/shard_map/all_to_all | solution.py:178
  19.8 0.2 fusion.11
  20.0 14.3 %all-to-all-done = bf16[32,7,8,128]{3,2,1,0:T(8,128)(2,1)S(1)} async-done(((bf16[32,7,8,128]{3,2,1,0:T(8,128)(2,1)}), bf16[32,7,8,128]{3,2,1,0:T(8,128)(2,1)S(1)}, u32[]{:S(2)}, u32[]{:S(2)}) %all-to-all-start) | async-done | bytes 458784 | tf_op jit(solution)/shard_map/all_to_all | solution.py:178
  34.3 0.2 dot_general.24
  34.5 0.1 reshape.37
  34.6 0.2 fusion.3
  34.8 0.9 %copy.27 = f32[64,2,512]{2,1,0:T(2,128)} copy(f32[64,2,512]{2,0,1:T(8,128)S(1)} %fusion.3) | data formatting | bytes 524288 | tf_op jit(solution)/shard_map/add | solution.py:192
  (21 shorter events, 0.4 us)
Async XLA Ops:
  0.0 19.7 %copy-start = (bf16[32,2,512]{2,1,0:T(2,128)(2,1)S(1)}, bf16[32,2,512]{2,1,0:T(2,128)(2,1)}, u32[]{:S(2)}) copy-start(bf16[32,2,512]{2,1,0:T(2,128)(2,1)} %param.18) | copy-start | bytes 196612
  0.0 8.0 %collective-permute-start = (bf16[2,2,16384]{2,1,0:T(2,128)(2,1)}, bf16[2,2,16384]{2,1,0:T(2,128)(2,1)S(1)}, u32[]{:S(2)}, u32[]{:S(2)}) collective-permute-start(bf16[2,2,16384]{2,1,0:T(2,128)(2,1)} %param.10), channel_id=1, source_target_pairs={{0,1},{1,0},{2,3},{3,2},{4,5},{5,4},{6,7},{7,6},{8,9},{9,8},{10,11... | collective-permute-start | bytes 393224 | tf_op jit(solution)/shard_map/ppermute | solution.py:154
  3.5 0.7 %copy-start.4 = (f32[256]{0:T(256)S(1)}, f32[256]{0:T(256)}, u32[]{:S(2)}) copy-start(f32[256]{0:T(256)} %param.11) | copy-start | bytes 3076
  5.1 2.8 %copy-start.1 = (bf16[2,2,16384]{2,1,0:T(2,128)(2,1)S(1)}, bf16[2,2,16384]{2,1,0:T(2,128)(2,1)}, u32[]{:S(2)}) copy-start(bf16[2,2,16384]{2,1,0:T(2,128)(2,1)} %param.10) | copy-start | bytes 393220
  5.3 0.7 %copy-start.3 = (f32[1,128,2]{1,2,0:T(2,128)S(1)}, f32[1,128,2]{1,2,0:T(2,128)}, u32[]{:S(2)}) copy-start(f32[1,128,2]{1,2,0:T(2,128)} %param.12) | copy-start | bytes 3076
  6.7 0.7 %copy-start.5 = (f32[1,128]{1,0:T(1,128)S(1)}, f32[1,128]{1,0:T(1,128)}, u32[]{:S(2)}) copy-start(f32[1,128]{1,0:T(1,128)} %param.16) | copy-start | bytes 1540
  14.1 5.6 %copy-start.2 = (bf16[64,32]{0,1:T(8,128)(2,1)S(1)}, bf16[64,32]{0,1:T(8,128)(2,1)}, u32[]{:S(2)}) copy-start(bf16[64,32]{0,1:T(8,128)(2,1)} %param.19) | copy-start | bytes 12292
  14.1 20.1 %all-to-all-start = ((bf16[32,7,8,128]{3,2,1,0:T(8,128)(2,1)}), bf16[32,7,8,128]{3,2,1,0:T(8,128)(2,1)S(1)}, u32[]{:S(2)}, u32[]{:S(2)}) async-start(bf16[32,7,8,128]{3,2,1,0:T(8,128)(2,1)} %bitcast.74), calls=%async_computation | async-start | bytes 917504 | tf_op jit(solution)/shard_map/all_to_all | solution.py:178

commit v11 on v9

--- a/solution.py
+++ b/solution.py
@@ -154,7 +154,7 @@
     else:
         raw_echo = lax.all_gather(echo, "range", axis=2, tiled=True)
     pulses, planes, bin_total = raw_echo.shape
-    chunk_total = bin_total // LANE + 2 * GROUP
+    chunk_total = bin_total // LANE + GROUP
     prof = compress_chunks(raw_echo, filter_matrix, chunk_total)
 
     starts = rec_start[0]

time: 35.7 us -> 35.7 us (level)
  no operation moved by 1% of the time
where the time goes in v11:
time: 35.7 us; the launch traced here: 35.4 us
  waiting for transfers between devices  14.3 us (40%)
  starting transfers between devices  8.23 us (23%)
  local copies, waits for them, and re-layouts  4.38 us (12%)
  Pallas kernels  3.97 us (11%)
  other arithmetic  1.96 us (5%)
  matrix products  1.66 us (5%)
  between operations  0.94 us (3%)
    all_to_all x1, waiting for transfers between devices, on_device(): lax.all_to_all(outgoing.reshape(owner_total, per_owner, GROUP, LANE), axe...  14.3 us
    all_to_all x1, starting transfers between devices, on_device(): lax.all_to_all(outgoing.reshape(owner_total, per_owner, GROUP, LANE), axe...  6.17 us
    pallas_call x1, Pallas kernels, form_payload(): pl.pallas_call(kernel, out_shape=jax.ShapeDtypeStruct((owner_total * (cap...  3.97 us
    ppermute x1, starting transfers between devices, on_device(): other = lax.ppermute(echo, 'range', [(0, 1), (1, 0)])  2.06 us
    dot_general x1, matrix products, compress_chunks(): jnp.dot(windows, filter_matrix, preferred_element_type=jnp.float32)  1.23 us
    another operation x4, local copies, waits for them, and re-layouts, banded(): jnp.tile(padded, tap_count)[:2 * tap_count * tap_count]  1.18 us
    add x1, local copies, waits for them, and re-layouts, on_device(): return fine + gathered  0.91 us
    mul x1, other arithmetic, chirp_matrix(): imag_taps = jnp.sin(chirp_phase) * tap_scale  0.72 us
  transfers between devices with their start and end apart: 2, of which 1 were waited for; matrix products, arithmetic and copies ran while one was open for 9% of the time, Pallas kernels for 0%

profile of v11, /device:TPU:1, one launch (start us, length us, event | category | flops | bytes accessed | tf_op | source)
XLA Modules:
  0.0 35.4 jit_solution(12623614307014901329)
XLA Ops:
  0.0 0.0 copy-start
  0.0 2.1 %collective-permute-start = (bf16[2,2,16384]{2,1,0:T(2,128)(2,1)}, bf16[2,2,16384]{2,1,0:T(2,128)(2,1)S(1)}, u32[]{:S(2)}, u32[]{:S(2)}) collective-permute-start(bf16[2,2,16384]{2,1,0:T(2,128)(2,1)} %param.10), channel_id=1, source_target_pairs={{0,1},{1,0},{2,3},{3,2},{4,5},{5,4},{6,7},{7,6},{8,9},{9,8},{10,11... | collective-permute-start | bytes 393224 | tf_op jit(solution)/shard_map/ppermute | solution.py:149
  2.1 0.7 %sine_multiply_fusion = f32[256]{0:T(256)S(1)} fusion(f32[256]{0:T(256)} %param.11), kind=kLoop, calls=%fused_computation.30 | loop fusion | flops 256 | bytes 2048 | tf_op jit(solution)/shard_map/mul | solution.py:19
  2.8 0.5 %tile.21 = f32[131328]{0:T(1024)S(1)} reshape(f32[256,513]{1,0:T(8,128)S(1)} %tile.20) | data formatting | bytes 1050624 | tf_op jit(solution)/shard_map/tile | solution.py:24
  3.4 0.0 copy-start.4
  3.4 0.0 copy-start.3
  3.4 0.1 reshape.39
  3.6 0.5 %copy-done.4 = f32[256]{0:T(256)S(1)} copy-done((f32[256]{0:T(256)S(1)}, f32[256]{0:T(256)}, u32[]{:S(2)}) %copy-start.4) | copy-done | bytes 1048
  4.1 0.0 copy-done.3
  4.9 0.0 copy-start.5
  4.9 0.0 copy-start.1
  4.9 0.6 %tile.9 = bf16[131328]{0:T(1024)(128)(2,1)S(1)} reshape(bf16[256,513]{1,0:T(8,128)(2,1)S(1)} %tile.8) | data formatting | bytes 525312 | tf_op jit(solution)/shard_map/tile | solution.py:24
  5.5 0.2 reshape.38
  5.8 0.6 %maximum_multiply_fusion.coef_ref = f32[4,128]{1,0:T(4,128)} fusion(f32[1,128]{1,0:T(1,128)S(1)} %get-tuple-element.16, f32[1,128]{1,0:T(1,128)S(1)} %get-tuple-element.11, f32[1,128]{1,0:T(1,128)S(1)} %get-tuple-element.17, f32[1,128]{1,0:T(1,128)S(1)} %get-tuple-element.10, f32[128]{0:T(128)S(1)} %fusion.18), kind=kLoop, calls=%fused_computation.28 | loop fusion | flops 2048 | bytes 4608 | tf_op jit(solution)/shard_map/mul | solution.py:168
  6.4 0.0 collective-permute-done
  6.4 0.0 copy-done.1
  6.4 0.2 broadcast_select_fusion.1
  6.6 0.2 fusion.11
  6.8 0.2 reshape.36
  7.0 0.1 fusion.20
  7.2 0.1 maximum_bitcast_fusion
  7.3 0.6 %copy.14 = bf16[2,264,2,384]{3,2,1,0:T(2,128)(2,1)S(1)} copy(bf16[2,264,2,384]{3,1,2,0:T(8,128)(2,1)S(1)} %maximum_bitcast_fusion) | data formatting | bytes 1622016 | tf_op jit(solution)/shard_map/transpose | solution.py:47
  7.9 0.1 copy.19
  8.0 1.2 %convolution_reduce-precision_fusion = f32[528,256]{1,0:T(8,128)} fusion(bf16[528,768]{1,0:T(8,128)(2,1)S(1)} %bitcast.51, bf16[384,128]{0,1:T(8,128)(2,1)S(1)} %slice.70, bf16[384,128]{0,1:T(8,128)(2,1)S(1)} %slice.71, bf16[384,128]{0,1:T(8,128)(2,1)S(1)} %negate_convert_fusion), kind=kOutput, calls=%fused_computation | convolution fusion | flops 209326080 | bytes 1646592 | tf_op jit(solution)/shard_map/dot_general | solution.py:48
  9.3 4.0 %shard_map.100 = bf16[224,8,128]{2,1,0:T(8,128)(2,1)} custom-call(s32[128]{0:T(128)} %bitcast.56, s32[128]{0:T(128)} %bitcast.57, s32[128]{0:T(128)} %bitcast.58, f32[4,128]{1,0:T(4,128)} %maximum_multiply_fusion.coef_ref, f32[2,264,256]{2,1,0:T(8,128)} %bitcast.52), custom_call_target="tpu_custom_call" | custom-call | tf_op jit(solution)/shard_map/pallas_call | solution.py:111
  13.2 6.2 %all-to-all-start = ((bf16[32,7,8,128]{3,2,1,0:T(8,128)(2,1)}), bf16[32,7,8,128]{3,2,1,0:T(8,128)(2,1)S(1)}, u32[]{:S(2)}, u32[]{:S(2)}) async-start(bf16[32,7,8,128]{3,2,1,0:T(8,128)(2,1)} %bitcast.48), calls=%async_computation | async-start | bytes 917504 | tf_op jit(solution)/shard_map/all_to_all | solution.py:173
  19.4 0.2 fusion.12
  19.7 14.3 %all-to-all-done = bf16[32,7,8,128]{3,2,1,0:T(8,128)(2,1)S(1)} async-done(((bf16[32,7,8,128]{3,2,1,0:T(8,128)(2,1)}), bf16[32,7,8,128]{3,2,1,0:T(8,128)(2,1)S(1)}, u32[]{:S(2)}, u32[]{:S(2)}) %all-to-all-start) | async-done | bytes 458784 | tf_op jit(solution)/shard_map/all_to_all | solution.py:173
  34.0 0.2 dot_general.16
  34.2 0.1 reshape.42
  34.3 0.2 fusion
  34.5 0.9 %copy.17 = f32[64,2,512]{2,1,0:T(2,128)} copy(f32[64,2,512]{2,0,1:T(8,128)S(1)} %fusion) | data formatting | bytes 524288 | tf_op jit(solution)/shard_map/add | solution.py:187
  (21 shorter events, 0.3 us)
Async XLA Ops:
  0.0 19.4 %copy-start = (bf16[32,2,512]{2,1,0:T(2,128)(2,1)S(1)}, bf16[32,2,512]{2,1,0:T(2,128)(2,1)}, u32[]{:S(2)}) copy-start(bf16[32,2,512]{2,1,0:T(2,128)(2,1)} %param.18) | copy-start | bytes 196612
  0.0 6.4 %collective-permute-start = (bf16[2,2,16384]{2,1,0:T(2,128)(2,1)}, bf16[2,2,16384]{2,1,0:T(2,128)(2,1)S(1)}, u32[]{:S(2)}, u32[]{:S(2)}) collective-permute-start(bf16[2,2,16384]{2,1,0:T(2,128)(2,1)} %param.10), channel_id=1, source_target_pairs={{0,1},{1,0},{2,3},{3,2},{4,5},{5,4},{6,7},{7,6},{8,9},{9,8},{10,11... | collective-permute-start | bytes 393224 | tf_op jit(solution)/shard_map/ppermute | solution.py:149
  3.4 0.7 %copy-start.4 = (f32[256]{0:T(256)S(1)}, f32[256]{0:T(256)}, u32[]{:S(2)}) copy-start(f32[256]{0:T(256)} %param.11) | copy-start | bytes 3076
  3.4 0.7 %copy-start.3 = (f32[1,128,2]{1,2,0:T(2,128)S(1)}, f32[1,128,2]{1,2,0:T(2,128)}, u32[]{:S(2)}) copy-start(f32[1,128,2]{1,2,0:T(2,128)} %param.12) | copy-start | bytes 3076
  4.9 0.9 %copy-start.5 = (f32[1,128]{1,0:T(1,128)S(1)}, f32[1,128]{1,0:T(1,128)}, u32[]{:S(2)}) copy-start(f32[1,128]{1,0:T(1,128)} %param.16) | copy-start | bytes 1540
  4.9 1.5 %copy-start.1 = (bf16[2,2,16384]{2,1,0:T(2,128)(2,1)S(1)}, bf16[2,2,16384]{2,1,0:T(2,128)(2,1)}, u32[]{:S(2)}) copy-start(bf16[2,2,16384]{2,1,0:T(2,128)(2,1)} %param.10) | copy-start | bytes 393220
  9.3 10.2 %copy-start.2 = (bf16[64,32]{0,1:T(8,128)(2,1)S(1)}, bf16[64,32]{0,1:T(8,128)(2,1)}, u32[]{:S(2)}) copy-start(bf16[64,32]{0,1:T(8,128)(2,1)} %param.19) | copy-start | bytes 12292
  13.2 20.7 %all-to-all-start = ((bf16[32,7,8,128]{3,2,1,0:T(8,128)(2,1)}), bf16[32,7,8,128]{3,2,1,0:T(8,128)(2,1)S(1)}, u32[]{:S(2)}, u32[]{:S(2)}) async-start(bf16[32,7,8,128]{3,2,1,0:T(8,128)(2,1)} %bitcast.48), calls=%async_computation | async-start | bytes 917504 | tf_op jit(solution)/shard_map/all_to_all | solution.py:173
